TPU v7x, 32 devices: a whole 2x2x4 slice. The times are simulated.
32 devices in a mesh: area: 4 (over x, core), sub: 8 (over z, y).
Axes of the slice: x: 2, y: 2, z: 4, core: 2. Of those that a mesh axis runs over, the one named last changes fastest.
Arguments:
- blocks: float32 [4, 512, 64, 256], P('area', 'sub'), as said below
- pattern: int32 [4, 512, 4], P('area', 'sub'), may hold values from 0 to 511, as said below
- line_ends: int32 [4, 2, 64], P('area'), may hold values from 0 to 32767, as said below
- sources: float32 [4, 4, 32768], P(None, 'area', 'sub'), may hold values from -6 to 6
- capacity: float32 [4, 32768], P('area', 'sub'), may hold values from 0.2 to 2
- start_volt: float32 [4, 32768], P('area', 'sub'), may hold values from -6 to 6
- start_hist: float32 [4, 2, 64], P('area'), may hold values from -6 to 6
- surge: float32 [4, 64], P('area'), may hold values from 0.2 to 1
Outputs:
- volt: float32 [4, 32768], P('area', 'sub')
- hist: float32 [4, 2, 64], P('area')
Inputs may be any that keep to these rules, and one draw needn't show every extreme that they name: pattern[a, r, 0] = r. Split the 512 block rows of an area into aligned groups of 64: the other entries of a row never point into the row's own group, no two of them in one group are equal, and the entries of one group point into between 27 and 28 distinct block rows of each other group, exactly 28 for some group. `line_ends`: within an area the line-end buses are distinct and rise from the first left end to the last right end. `blocks`: the diagonal of each first stored block lies in 2 to 4.
All inputs are finite; a program needn't handle non-finite values.
Results may differ from a plain program's by a relative error of at most 0.00011.
Values sent between devices are 32-bit elements; how exact they have to be, the bound alone decides.
No kernel may reach another device: no remote copies, remote signals or barrier semaphores. Data moves between devices by JAX's collectives and lax.ppermute only.
A program may use at most 64 MiB of HBM per device.

v0:
```python
import jax
import jax.numpy as jnp
from jax import lax
from jax.sharding import PartitionSpec as P

STEPS = 4
SWEEPS = 8


def shifted(value, axis, steps):
    count = lax.axis_size(axis)
    pairs = [(source, (source + steps) % count) for source in range(count)]
    return lax.ppermute(value, axis, pairs)


def collect(field):
    return lax.all_gather(field, "sub", axis=1, tiled=True)


def apply_blocks(blocks, own_part, others):
    picked = jnp.concatenate([own_part, others], axis=1)
    result = jnp.einsum("rik,rk->ri", blocks[0], picked, precision=lax.Precision.HIGHEST)
    return result.reshape(1, -1)


def on_device(blocks, pattern, line_ends, sources, capacity, start_volt, start_hist, surge):
    width = blocks.shape[2]
    rows_here = blocks.shape[1]
    local_count = rows_here * width
    offset = lax.axis_index("sub") * local_count
    diag = jnp.diagonal(blocks[..., :width], axis1=2, axis2=3).reshape(1, local_count)
    system_diag = diag + capacity
    remote_cols = pattern[0][:, 1:].reshape(-1)
    local_ends = line_ends - offset
    inside = (local_ends >= 0) & (local_ends < local_count)
    safe_ends = jnp.clip(local_ends, 0, local_count - 1)
    volt = start_volt
    hist = start_hist
    carried = []
    for step in range(STEPS):
        rhs = sources[step] + capacity * volt
        inject = jnp.where(inside, -hist, 0.0)
        rhs = rhs.at[0, safe_ends.reshape(-1)].add(inject.reshape(-1))
        field = volt
        for sweep in range(SWEEPS):
            own_part = field.reshape(rows_here, width)
            whole = collect(field)
            others = whole.reshape(-1, width)[remote_cols]
            others = others.reshape(rows_here, -1)
            result = apply_blocks(blocks, own_part, others)
            field = field + (rhs - result - capacity * field) / system_diag
        volt = field
        partial_volt = jnp.where(inside, volt[0][safe_ends[0]][None], 0.0)
        end_volt = lax.psum(partial_volt, "sub")
        message = -2.0 * surge * end_volt[:, 1] - hist[:, 1]
        new_left = shifted(message, "area", 1)
        outgoing_ends = jnp.stack([end_volt[:, 0], hist[:, 0]], axis=1)
        from_right = shifted(outgoing_ends, "area", -1)
        new_right = -2.0 * surge * from_right[:, 0] - from_right[:, 1]
        hist = jnp.stack([new_left, new_right], axis=1)
    return (volt, hist)


def solution(mesh):
    in_specs = (
        P("area", "sub", None, None),
        P("area", "sub", None),
        P("area", None, None),
        P(None, "area", "sub"),
        P("area", "sub"),
        P("area", "sub"),
        P("area", None, None),
        P("area", None),
    )
    out_specs = (P("area", "sub"), P("area", None, None))
    return jax.shard_map(
        on_device, mesh=mesh, in_specs=in_specs, out_specs=out_specs, check_vma=False
    )
```

profile of v0, /device:TPU:0, one launch (start us, length us, event | category | flops | bytes accessed | tf_op | source)
XLA Modules:
  0.0 1362.5 jit_solution(36075500390137617)
XLA Ops:
  2.0 32.5 %all_gather.96 = f32[1,32768]{1,0:T(1,128)S(1)} all-gather(f32[1,4096]{1,0:T(1,128)} %param.13), channel_id=1, replica_groups=mesh['area'=4,'sub'=8] {'sub'}, dimensions={1}, use_global_device_ids=true | all-gather | bytes 147456 | tf_op jit(solution)/shard_map/all_gather | solution.py:17
  51.7 30.5 %all_gather.97 = f32[1,32768]{1,0:T(1,128)S(1)} all-gather(f32[1,4096]{1,0:T(1,128)S(1)} %get-tuple-element.71), channel_id=1, replica_groups=mesh['area'=4,'sub'=8] {'sub'}, dimensions={1}, use_global_device_ids=true | all-gather | bytes 147456 | tf_op jit(solution)/shard_map/all_gather | solution.py:17
  84.2 5.7 fusion.60
  90.7 30.7 %all_gather.98 = f32[1,32768]{1,0:T(1,128)S(1)} all-gather(f32[1,4096]{1,0:T(1,128)S(1)} %get-tuple-element.69), channel_id=1, replica_groups=mesh['area'=4,'sub'=8] {'sub'}, dimensions={1}, use_global_device_ids=true | all-gather | bytes 147456 | tf_op jit(solution)/shard_map/all_gather | solution.py:17
  123.5 5.7 fusion.58
  130.0 30.5 %all_gather.99 = f32[1,32768]{1,0:T(1,128)S(1)} all-gather(f32[1,4096]{1,0:T(1,128)S(1)} %get-tuple-element.67), channel_id=1, replica_groups=mesh['area'=4,'sub'=8] {'sub'}, dimensions={1}, use_global_device_ids=true | all-gather | bytes 147456 | tf_op jit(solution)/shard_map/all_gather | solution.py:17
  162.5 5.7 fusion.56
  169.1 30.5 %all_gather.100 = f32[1,32768]{1,0:T(1,128)S(1)} all-gather(f32[1,4096]{1,0:T(1,128)S(1)} %get-tuple-element.65), channel_id=1, replica_groups=mesh['area'=4,'sub'=8] {'sub'}, dimensions={1}, use_global_device_ids=true | all-gather | bytes 147456 | tf_op jit(solution)/shard_map/all_gather | solution.py:17
  201.6 5.7 fusion.54
  208.2 30.9 %all_gather.101 = f32[1,32768]{1,0:T(1,128)S(1)} all-gather(f32[1,4096]{1,0:T(1,128)S(1)} %get-tuple-element.63), channel_id=1, replica_groups=mesh['area'=4,'sub'=8] {'sub'}, dimensions={1}, use_global_device_ids=true | all-gather | bytes 147456 | tf_op jit(solution)/shard_map/all_gather | solution.py:17
  241.1 5.7 fusion.52
  247.7 30.5 %all_gather.102 = f32[1,32768]{1,0:T(1,128)S(1)} all-gather(f32[1,4096]{1,0:T(1,128)S(1)} %get-tuple-element.61), channel_id=1, replica_groups=mesh['area'=4,'sub'=8] {'sub'}, dimensions={1}, use_global_device_ids=true | all-gather | bytes 147456 | tf_op jit(solution)/shard_map/all_gather | solution.py:17
  280.2 5.7 fusion.50
  286.7 30.5 %all_gather.103 = f32[1,32768]{1,0:T(1,128)S(1)} all-gather(f32[1,4096]{1,0:T(1,128)S(1)} %get-tuple-element.59), channel_id=1, replica_groups=mesh['area'=4,'sub'=8] {'sub'}, dimensions={1}, use_global_device_ids=true | all-gather | bytes 147456 | tf_op jit(solution)/shard_map/all_gather | solution.py:17
  319.3 5.7 fusion.48
  327.2 21.3 %psum.28 = f32[1,2,64]{2,1,0:T(2,128)S(1)} all-reduce(f32[1,2,64]{2,1,0:T(2,128)S(1)} %broadcast_select_fusion.3), channel_id=1, replica_groups=mesh['area'=4,'sub'=8] {'sub'}, use_global_device_ids=true, to_apply=%region_1.2 | all-reduce | flops 128 | bytes 1024 | tf_op jit(solution)/shard_map/psum | solution.py:54
  348.8 30.5 %all_gather.104 = f32[1,32768]{1,0:T(1,128)S(1)} all-gather(f32[1,4096]{1,0:T(1,128)S(1)} %get-tuple-element.53), channel_id=1, replica_groups=mesh['area'=4,'sub'=8] {'sub'}, dimensions={1}, use_global_device_ids=true | all-gather | bytes 147456 | tf_op jit(solution)/shard_map/all_gather | solution.py:17
  381.4 5.7 fusion.46
  389.5 30.5 %all_gather.105 = f32[1,32768]{1,0:T(1,128)S(1)} all-gather(f32[1,4096]{1,0:T(1,128)S(1)} %get-tuple-element.51), channel_id=1, replica_groups=mesh['area'=4,'sub'=8] {'sub'}, dimensions={1}, use_global_device_ids=true | all-gather | bytes 147456 | tf_op jit(solution)/shard_map/all_gather | solution.py:17
  422.2 5.7 fusion.44
  428.8 30.7 %all_gather.106 = f32[1,32768]{1,0:T(1,128)S(1)} all-gather(f32[1,4096]{1,0:T(1,128)S(1)} %get-tuple-element.49), channel_id=1, replica_groups=mesh['area'=4,'sub'=8] {'sub'}, dimensions={1}, use_global_device_ids=true | all-gather | bytes 147456 | tf_op jit(solution)/shard_map/all_gather | solution.py:17
  461.6 5.7 fusion.42
  468.2 30.6 %all_gather.107 = f32[1,32768]{1,0:T(1,128)S(1)} all-gather(f32[1,4096]{1,0:T(1,128)S(1)} %get-tuple-element.47), channel_id=1, replica_groups=mesh['area'=4,'sub'=8] {'sub'}, dimensions={1}, use_global_device_ids=true | all-gather | bytes 147456 | tf_op jit(solution)/shard_map/all_gather | solution.py:17
  500.9 5.7 fusion.40
  507.5 30.6 %all_gather.108 = f32[1,32768]{1,0:T(1,128)S(1)} all-gather(f32[1,4096]{1,0:T(1,128)S(1)} %get-tuple-element.45), channel_id=1, replica_groups=mesh['area'=4,'sub'=8] {'sub'}, dimensions={1}, use_global_device_ids=true | all-gather | bytes 147456 | tf_op jit(solution)/shard_map/all_gather | solution.py:17
  540.2 5.7 fusion.38
  546.7 30.9 %all_gather.109 = f32[1,32768]{1,0:T(1,128)S(1)} all-gather(f32[1,4096]{1,0:T(1,128)S(1)} %get-tuple-element.43), channel_id=1, replica_groups=mesh['area'=4,'sub'=8] {'sub'}, dimensions={1}, use_global_device_ids=true | all-gather | bytes 147456 | tf_op jit(solution)/shard_map/all_gather | solution.py:17
  579.8 5.7 fusion.36
  586.3 30.5 %all_gather.110 = f32[1,32768]{1,0:T(1,128)S(1)} all-gather(f32[1,4096]{1,0:T(1,128)S(1)} %get-tuple-element.41), channel_id=1, replica_groups=mesh['area'=4,'sub'=8] {'sub'}, dimensions={1}, use_global_device_ids=true | all-gather | bytes 147456 | tf_op jit(solution)/shard_map/all_gather | solution.py:17
  619.0 5.7 fusion.34
  625.6 30.5 %all_gather.111 = f32[1,32768]{1,0:T(1,128)S(1)} all-gather(f32[1,4096]{1,0:T(1,128)S(1)} %get-tuple-element.39), channel_id=1, replica_groups=mesh['area'=4,'sub'=8] {'sub'}, dimensions={1}, use_global_device_ids=true | all-gather | bytes 147456 | tf_op jit(solution)/shard_map/all_gather | solution.py:17
  658.2 5.7 fusion.32
  664.8 30.7 %all_gather.112 = f32[1,32768]{1,0:T(1,128)S(1)} all-gather(f32[1,4096]{1,0:T(1,128)S(1)} %get-tuple-element.35), channel_id=1, replica_groups=mesh['area'=4,'sub'=8] {'sub'}, dimensions={1}, use_global_device_ids=true | all-gather | bytes 147456 | tf_op jit(solution)/shard_map/all_gather | solution.py:17
  698.7 17.1 %psum.29 = f32[1,2,64]{2,1,0:T(2,128)S(1)} all-reduce(f32[1,2,64]{2,1,0:T(2,128)S(1)} %broadcast_select_fusion.2), channel_id=1, replica_groups=mesh['area'=4,'sub'=8] {'sub'}, use_global_device_ids=true, to_apply=%region_3.4 | all-reduce | flops 128 | bytes 1024 | tf_op jit(solution)/shard_map/psum | solution.py:54
  726.9 30.6 %all_gather.113 = f32[1,32768]{1,0:T(1,128)S(1)} all-gather(f32[1,4096]{1,0:T(1,128)S(1)} %get-tuple-element.33), channel_id=1, replica_groups=mesh['area'=4,'sub'=8] {'sub'}, dimensions={1}, use_global_device_ids=true | all-gather | bytes 147456 | tf_op jit(solution)/shard_map/all_gather | solution.py:17
  759.6 5.7 fusion.28
  766.2 30.8 %all_gather.114 = f32[1,32768]{1,0:T(1,128)S(1)} all-gather(f32[1,4096]{1,0:T(1,128)S(1)} %get-tuple-element.31), channel_id=1, replica_groups=mesh['area'=4,'sub'=8] {'sub'}, dimensions={1}, use_global_device_ids=true | all-gather | bytes 147456 | tf_op jit(solution)/shard_map/all_gather | solution.py:17
  799.1 5.7 fusion.26
  805.7 30.5 %all_gather.115 = f32[1,32768]{1,0:T(1,128)S(1)} all-gather(f32[1,4096]{1,0:T(1,128)S(1)} %get-tuple-element.29), channel_id=1, replica_groups=mesh['area'=4,'sub'=8] {'sub'}, dimensions={1}, use_global_device_ids=true | all-gather | bytes 147456 | tf_op jit(solution)/shard_map/all_gather | solution.py:17
  838.3 5.7 fusion.24
  844.9 30.6 %all_gather.116 = f32[1,32768]{1,0:T(1,128)S(1)} all-gather(f32[1,4096]{1,0:T(1,128)S(1)} %get-tuple-element.27), channel_id=1, replica_groups=mesh['area'=4,'sub'=8] {'sub'}, dimensions={1}, use_global_device_ids=true | all-gather | bytes 147456 | tf_op jit(solution)/shard_map/all_gather | solution.py:17
  877.6 5.7 fusion.22
  884.1 30.9 %all_gather.117 = f32[1,32768]{1,0:T(1,128)S(1)} all-gather(f32[1,4096]{1,0:T(1,128)S(1)} %get-tuple-element.25), channel_id=1, replica_groups=mesh['area'=4,'sub'=8] {'sub'}, dimensions={1}, use_global_device_ids=true | all-gather | bytes 147456 | tf_op jit(solution)/shard_map/all_gather | solution.py:17
  917.2 5.7 fusion.20
  923.8 30.5 %all_gather.118 = f32[1,32768]{1,0:T(1,128)S(1)} all-gather(f32[1,4096]{1,0:T(1,128)S(1)} %get-tuple-element.23), channel_id=1, replica_groups=mesh['area'=4,'sub'=8] {'sub'}, dimensions={1}, use_global_device_ids=true | all-gather | bytes 147456 | tf_op jit(solution)/shard_map/all_gather | solution.py:17
  956.4 5.7 fusion.18
  963.0 30.5 %all_gather.119 = f32[1,32768]{1,0:T(1,128)S(1)} all-gather(f32[1,4096]{1,0:T(1,128)S(1)} %get-tuple-element.21), channel_id=1, replica_groups=mesh['area'=4,'sub'=8] {'sub'}, dimensions={1}, use_global_device_ids=true | all-gather | bytes 147456 | tf_op jit(solution)/shard_map/all_gather | solution.py:17
  995.6 5.7 fusion.16
  1002.2 30.7 %all_gather.120 = f32[1,32768]{1,0:T(1,128)S(1)} all-gather(f32[1,4096]{1,0:T(1,128)S(1)} %get-tuple-element.17), channel_id=1, replica_groups=mesh['area'=4,'sub'=8] {'sub'}, dimensions={1}, use_global_device_ids=true | all-gather | bytes 147456 | tf_op jit(solution)/shard_map/all_gather | solution.py:17
  1036.1 19.1 %psum.30 = f32[1,2,64]{2,1,0:T(2,128)S(1)} all-reduce(f32[1,2,64]{2,1,0:T(2,128)S(1)} %broadcast_select_fusion.1), channel_id=1, replica_groups=mesh['area'=4,'sub'=8] {'sub'}, use_global_device_ids=true, to_apply=%region_5.6 | all-reduce | flops 128 | bytes 1024 | tf_op jit(solution)/shard_map/psum | solution.py:54
  1065.2 30.6 %all_gather.121 = f32[1,32768]{1,0:T(1,128)S(1)} all-gather(f32[1,4096]{1,0:T(1,128)S(1)} %get-tuple-element.15), channel_id=1, replica_groups=mesh['area'=4,'sub'=8] {'sub'}, dimensions={1}, use_global_device_ids=true | all-gather | bytes 147456 | tf_op jit(solution)/shard_map/all_gather | solution.py:17
  1097.8 5.7 fusion.12
  1104.3 30.8 %all_gather.122 = f32[1,32768]{1,0:T(1,128)S(1)} all-gather(f32[1,4096]{1,0:T(1,128)S(1)} %get-tuple-element.13), channel_id=1, replica_groups=mesh['area'=4,'sub'=8] {'sub'}, dimensions={1}, use_global_device_ids=true | all-gather | bytes 147456 | tf_op jit(solution)/shard_map/all_gather | solution.py:17
  1137.1 5.7 fusion.10
  1143.7 30.6 %all_gather.123 = f32[1,32768]{1,0:T(1,128)S(1)} all-gather(f32[1,4096]{1,0:T(1,128)S(1)} %get-tuple-element.11), channel_id=1, replica_groups=mesh['area'=4,'sub'=8] {'sub'}, dimensions={1}, use_global_device_ids=true | all-gather | bytes 147456 | tf_op jit(solution)/shard_map/all_gather | solution.py:17
  1176.3 5.7 fusion.8
  1182.8 30.6 %all_gather.124 = f32[1,32768]{1,0:T(1,128)S(1)} all-gather(f32[1,4096]{1,0:T(1,128)S(1)} %get-tuple-element.9), channel_id=1, replica_groups=mesh['area'=4,'sub'=8] {'sub'}, dimensions={1}, use_global_device_ids=true | all-gather | bytes 147456 | tf_op jit(solution)/shard_map/all_gather | solution.py:17
  1215.4 5.7 fusion.6
  1222.0 30.8 %all_gather.125 = f32[1,32768]{1,0:T(1,128)S(1)} all-gather(f32[1,4096]{1,0:T(1,128)S(1)} %get-tuple-element.7), channel_id=1, replica_groups=mesh['area'=4,'sub'=8] {'sub'}, dimensions={1}, use_global_device_ids=true | all-gather | bytes 147456 | tf_op jit(solution)/shard_map/all_gather | solution.py:17
  1254.7 5.7 fusion.4
  1261.3 30.5 %all_gather.126 = f32[1,32768]{1,0:T(1,128)S(1)} all-gather(f32[1,4096]{1,0:T(1,128)S(1)} %get-tuple-element.5), channel_id=1, replica_groups=mesh['area'=4,'sub'=8] {'sub'}, dimensions={1}, use_global_device_ids=true | all-gather | bytes 147456 | tf_op jit(solution)/shard_map/all_gather | solution.py:17
  1293.8 5.7 fusion.2
  1300.4 30.5 %all_gather.127 = f32[1,32768]{1,0:T(1,128)S(1)} all-gather(f32[1,4096]{1,0:T(1,128)S(1)} %get-tuple-element.3), channel_id=1, replica_groups=mesh['area'=4,'sub'=8] {'sub'}, dimensions={1}, use_global_device_ids=true | all-gather | bytes 147456 | tf_op jit(solution)/shard_map/all_gather | solution.py:17
  1340.0 17.1 %psum.31 = f32[1,2,64]{2,1,0:T(2,128)S(1)} all-reduce(f32[1,2,64]{2,1,0:T(2,128)S(1)} %broadcast_select_fusion), channel_id=1, replica_groups=mesh['area'=4,'sub'=8] {'sub'}, use_global_device_ids=true, to_apply=%region_7.8 | all-reduce | flops 128 | bytes 1024 | tf_op jit(solution)/shard_map/psum | solution.py:54
  (355 shorter events, 143.0 us)
Async XLA Ops:
  37.1 343.3 %copy-start.3 = (s32[1024]{0:T(1024)}, s32[1024]{0:T(1024)S(1)}, u32[]{:S(2)}) copy-start(s32[1024]{0:T(1024)S(1)} %pad_clamp_fusion.1) | copy-start | bytes 12292
  39.4 2.2 copy-start
  39.4 6.1 slice-start
  41.6 9.3 copy-start.2
  41.6 9.3 copy-start.5
  285.9 62.6 %slice-start.1 = ((f32[1,2,64]{2,1,0:T(2,128)}), f32[1,1,64]{2,1,0:T(1,128)S(1)}, s32[]{:S(2)}) async-start(f32[1,2,64]{2,1,0:T(2,128)} %param.14), calls=%async_computation.1 | async-start | bytes 1024 | tf_op jit(solution)/shard_map/slice | solution.py:57
  285.9 93.4 %copy-start.6 = (f32[4,1,4096]{2,1,0:T(1,128)S(1)}, f32[4,1,4096]{2,1,0:T(1,128)}, u32[]{:S(2)}) copy-start(f32[4,1,4096]{2,1,0:T(1,128)} %param.11) | copy-start | bytes 196612
  319.0 62.3 %copy-start.7 = (f32[1,64]{1,0:T(1,128)S(1)}, f32[1,64]{1,0:T(1,128)}, u32[]{:S(2)}) copy-start(f32[1,64]{1,0:T(1,128)} %param.15) | copy-start | bytes 772
  319.0 62.3 %copy-start.8 = (f32[1,2,64]{2,1,0:T(2,128)S(1)}, f32[1,2,64]{2,1,0:T(2,128)}, u32[]{:S(2)}) copy-start(f32[1,2,64]{2,1,0:T(2,128)} %param.14) | copy-start | bytes 1540
  348.5 32.8 %collective-permute-start.1 = (f32[1,2,64]{2,1,0:T(2,128)S(1)}, f32[1,2,64]{2,1,0:T(2,128)S(1)}, u32[]{:S(2)}, u32[]{:S(2)}) collective-permute-start(f32[1,2,64]{2,1,0:T(2,128)S(1)} %pad_maximum_fusion), channel_id=1, source_target_pairs={{0,24},{8,0},{16,8},{24,16},{1,25},{9,1},{17,9},{25,17},{2,26},{10... | collective-permute-start | bytes 1544 | tf_op jit(solution)/shard_map/ppermute | solution.py:13
  381.4 5.9 collective-permute-start
  624.7 71.8 %copy-start.4 = (s32[1024]{0:T(1024)S(1)}, s32[1024]{0:T(1024)}, u32[]{:S(2)}) copy-start(s32[1024]{0:T(1024)} %copy-done.3) | copy-start | bytes 12292
  715.8 1.4 collective-permute-start.3
  717.2 7.4 collective-permute-start.2
  1055.2 1.4 collective-permute-start.5
  1056.5 6.4 collective-permute-start.4
  1338.8 23.3 %copy-start.1 = (f32[1,4096]{1,0:T(1,128)}, f32[1,4096]{1,0:T(1,128)S(1)}, u32[]{:S(2)}) copy-start(f32[1,4096]{1,0:T(1,128)S(1)} %divide_add_fusion) | copy-start | bytes 49156
  1357.2 1.4 collective-permute-start.7
  1358.5 3.0 collective-permute-start.6
where the time goes:
time: 1370 us; the launch traced here: 1360 us
  blocking collectives  1060 us (77%)
  matrix products  181 us (13%)
  other arithmetic  64.7 us (5%)
  local copies, waits for them, and re-layouts  48.2 us (4%)
    all_gather x32, blocking collectives, collect(): return lax.all_gather(field, 'sub', axis=1, tiled=True)  982 us
    dot_general x32, matrix products, apply_blocks(): jnp.einsum('rik,rk->ri', blocks[0], picked, precision=lax.Precision.HIGHEST)  181 us
    psum x4, blocking collectives, on_device(): end_volt = lax.psum(partial_volt, 'sub')  74.6 us
    all_gather x32, other arithmetic, collect(): return lax.all_gather(field, 'sub', axis=1, tiled=True)  30.4 us
  transfers between devices with their start and end apart: 8, of which 4 were waited for; matrix products, arithmetic and copies ran while one was open for 1% of the time, Pallas kernels for 0%

commit v1 on v0

v1 whole, which is shorter than its diff:
```python
import jax
import jax.numpy as jnp
from jax import lax
from jax.sharding import PartitionSpec as P

STEPS = 4
SWEEPS = 8


def shifted(value, axis, steps):
    count = lax.axis_size(axis)
    pairs = [(source, (source + steps) % count) for source in range(count)]
    return lax.ppermute(value, axis, pairs)


def collect(value):
    count = lax.axis_size("sub")
    parts = [value] + [shifted(value, "sub", k) for k in range(1, count)]
    return jnp.stack(parts)


def rotated(index, me, count, chunk):
    owner = index // chunk
    slot = (me - owner) % count
    return slot * chunk + index % chunk


def apply_blocks(blocks, own_part, others):
    picked = jnp.concatenate([own_part, others], axis=1)
    result = jnp.einsum("rik,rk->ri", blocks[0], picked, precision=lax.Precision.HIGHEST)
    return result.reshape(1, -1)


def next_hist(end_volt, hist, surge):
    message = -2.0 * surge * end_volt[:, 1] - hist[:, 1]
    new_left = shifted(message, "area", 1)
    outgoing_ends = jnp.stack([end_volt[:, 0], hist[:, 0]], axis=1)
    from_right = shifted(outgoing_ends, "area", -1)
    new_right = -2.0 * surge * from_right[:, 0] - from_right[:, 1]
    return jnp.stack([new_left, new_right], axis=1)


def on_device(blocks, pattern, line_ends, sources, capacity, start_volt, start_hist, surge):
    width = blocks.shape[2]
    rows_here = blocks.shape[1]
    local_count = rows_here * width
    count = lax.axis_size("sub")
    me = lax.axis_index("sub")
    offset = me * local_count
    diag = jnp.diagonal(blocks[..., :width], axis1=2, axis2=3).reshape(1, local_count)
    system_diag = diag + capacity
    remote_cols = rotated(pattern[0][:, 1:].reshape(-1), me, count, rows_here)
    end_index = rotated(line_ends[0], me, count, local_count)
    local_ends = line_ends - offset
    inside = (local_ends >= 0) & (local_ends < local_count)
    safe_ends = jnp.clip(local_ends, 0, local_count - 1)
    volt = start_volt
    hist = start_hist
    for step in range(STEPS):
        field = volt
        rhs = None
        for sweep in range(SWEEPS):
            whole = collect(field)
            if rhs is None:
                if step > 0:
                    end_volt = whole.reshape(-1)[end_index][None]
                    hist = next_hist(end_volt, hist, surge)
                rhs = sources[step] + capacity * volt
                inject = jnp.where(inside, -hist, 0.0)
                rhs = rhs.at[0, safe_ends.reshape(-1)].add(inject.reshape(-1))
            own_part = field.reshape(rows_here, width)
            others = whole.reshape(-1, width)[remote_cols]
            others = others.reshape(rows_here, -1)
            result = apply_blocks(blocks, own_part, others)
            field = field + (rhs - result - capacity * field) / system_diag
        volt = field
    partial_volt = jnp.where(inside, volt[0][safe_ends[0]][None], 0.0)
    end_volt = jnp.sum(collect(partial_volt), axis=0)
    hist = next_hist(end_volt, hist, surge)
    return (volt, hist)


def solution(mesh):
    in_specs = (
        P("area", "sub", None, None),
        P("area", "sub", None),
        P("area", None, None),
        P(None, "area", "sub"),
        P("area", "sub"),
        P("area", "sub"),
        P("area", None, None),
        P("area", None),
    )
    out_specs = (P("area", "sub"), P("area", None, None))
    return jax.shard_map(
        on_device, mesh=mesh, in_specs=in_specs, out_specs=out_specs, check_vma=False
    )
```

time: 1370 us -> 740 us (0.54)
  blocking collectives: 1060 us -> 0 us
  starting transfers between devices: 4.36 us -> 374 us
  waiting for transfers between devices: 5 us -> 83.3 us
  other arithmetic: 64.7 us -> 34.3 us
    all_gather x32 -> x0, blocking collectives: 982 us -> none  [collect(): return lax.all_gather(field, 'sub', axis=1, tiled=True)]
    ppermute x8 -> x239, starting transfers between devices: 4.36 us -> 374 us  [shifted(): return lax.ppermute(value, axis, pairs)]
    ppermute x8 -> x239, waiting for transfers between devices: 5 us -> 83.3 us  [shifted(): return lax.ppermute(value, axis, pairs)]
    psum x4 -> x0, blocking collectives: 74.6 us -> none  [on_device(): end_volt = lax.psum(partial_volt, 'sub')]
    all_gather x32 -> x0, other arithmetic: 30.4 us -> none  [collect(): return lax.all_gather(field, 'sub', axis=1, tiled=True)]
  transfers between devices with their start and end apart: 8 -> 239, of which waited for: 4 -> 94; matrix products, arithmetic and copies ran while one was open for 1% -> 4% of each run, Pallas kernels for 0% -> 0%
where the time goes in v1:
time: 740 us; the launch traced here: 730 us
  starting transfers between devices  374 us (51%)
  matrix products  183 us (25%)
  waiting for transfers between devices  83.3 us (11%)
  local copies, waits for them, and re-layouts  52.5 us (7%)
  other arithmetic  34.3 us (5%)
    ppermute x239, starting transfers between devices, shifted(): return lax.ppermute(value, axis, pairs)  374 us
    dot_general x32, matrix products, apply_blocks(): jnp.einsum('rik,rk->ri', blocks[0], picked, precision=lax.Precision.HIGHEST)  183 us
    ppermute x239, waiting for transfers between devices, shifted(): return lax.ppermute(value, axis, pairs)  83.3 us
    gather x32, local copies, waits for them, and re-layouts, on_device(): others = whole.reshape(-1, width)[remote_cols]  24.2 us
    add x32, other arithmetic, on_device(): field = field + (rhs - result - capacity * field) / system_diag  22.3 us
  transfers between devices with their start and end apart: 239, of which 94 were waited for; matrix products, arithmetic and copies ran while one was open for 4% of the time, Pallas kernels for 0%

profile of v1, /device:TPU:0, one launch (start us, length us, event | category | flops | bytes accessed | tf_op | source)
XLA Modules:
  0.0 729.9 jit_solution(5444320912511597810)
XLA Ops:
  0.6 5.1 collective-permute-start.5
  14.1 4.5 collective-permute-start.3
  25.3 5.7 fusion.62
  31.9 2.9 collective-permute-start.7
  36.4 2.8 collective-permute-start.10
  39.4 3.1 collective-permute-start.12
  47.3 5.7 fusion.60
  68.4 5.7 fusion.58
  78.7 2.6 collective-permute-start.24
  81.3 3.6 collective-permute-start.25
  89.9 5.7 fusion.56
  100.5 3.3 collective-permute-start.31
  111.2 5.7 fusion.54
  121.5 3.1 collective-permute-start.38
  133.0 5.7 fusion.52
  154.0 5.7 fusion.50
  164.2 3.2 collective-permute-start.52
  175.5 5.7 fusion.48
  201.1 5.7 fusion.46
  213.1 2.8 collective-permute-start.68
  223.8 5.7 fusion.44
  234.3 3.1 collective-permute-start.75
  245.4 5.7 fusion.42
  255.7 2.9 collective-permute-start.82
  266.9 5.7 fusion.40
  288.1 5.7 fusion.38
  298.4 3.0 collective-permute-start.96
  309.4 5.7 fusion.36
  319.9 2.7 collective-permute-start.103
  330.9 5.7 fusion.34
  341.1 3.1 collective-permute-start.110
  352.1 5.7 fusion.32
  362.7 3.0 collective-permute-start.117
  377.1 5.7 fusion.30
  389.0 2.8 collective-permute-start.126
  400.0 5.7 fusion.28
  421.2 5.7 fusion.26
  431.5 3.1 collective-permute-start.140
  442.4 5.7 fusion.24
  452.9 2.7 collective-permute-start.147
  464.1 5.7 fusion.22
  474.4 2.9 collective-permute-start.154
  485.1 5.7 fusion.20
  495.8 2.8 collective-permute-start.161
  506.8 5.7 fusion.18
  517.1 2.8 collective-permute-start.168
  528.3 5.7 fusion.16
  541.2 2.7 collective-permute-start.176
  553.8 5.7 fusion.14
  565.8 3.1 collective-permute-start.184
  576.4 5.7 fusion.12
  586.9 2.7 collective-permute-start.191
  598.0 5.7 fusion.10
  608.3 2.7 collective-permute-start.198
  618.8 5.7 fusion.8
  629.3 3.0 collective-permute-start.205
  640.3 5.7 fusion.6
  650.7 2.7 collective-permute-start.212
  661.5 5.7 fusion.4
  671.9 2.9 collective-permute-start.219
  682.7 5.7 fusion.2
  693.3 2.9 collective-permute-start.226
  704.2 5.7 fusion
  715.1 2.7 collective-permute-start.233
  (782 shorter events, 446.9 us)
Async XLA Ops:
  0.6 13.5 %collective-permute-start.5 = (f32[1,4096]{1,0:T(1,128)}, f32[1,4096]{1,0:T(1,128)S(1)}, u32[]{:S(2)}, u32[]{:S(2)}) collective-permute-start(f32[1,4096]{1,0:T(1,128)} %param.13), channel_id=1, source_target_pairs={{0,6},{1,7},{2,0},{3,1},{4,2},{5,3},{6,4},{7,5},{8,14},{9,15},{10,... | collective-permute-start | bytes 49160 | tf_op jit(solution)/shard_map/ppermute | solution.py:13
  5.8 12.8 %collective-permute-start.6 = (f32[1,4096]{1,0:T(1,128)}, f32[1,4096]{1,0:T(1,128)S(1)}, u32[]{:S(2)}, u32[]{:S(2)}) collective-permute-start(f32[1,4096]{1,0:T(1,128)} %param.13), channel_id=1, source_target_pairs={{0,7},{1,0},{2,1},{3,2},{4,3},{5,4},{6,5},{7,6},{8,15},{9,8},{10,9... | collective-permute-start | bytes 49160 | tf_op jit(solution)/shard_map/ppermute | solution.py:13
  7.2 16.9 %collective-permute-start = (f32[1,4096]{1,0:T(1,128)}, f32[1,4096]{1,0:T(1,128)S(1)}, u32[]{:S(2)}, u32[]{:S(2)}) collective-permute-start(f32[1,4096]{1,0:T(1,128)} %param.13), channel_id=1, source_target_pairs={{0,1},{1,2},{2,3},{3,4},{4,5},{5,6},{6,7},{7,0},{8,9},{9,10},{10,1... | collective-permute-start | bytes 49160 | tf_op jit(solution)/shard_map/ppermute | solution.py:13
  7.8 16.3 %collective-permute-start.1 = (f32[1,4096]{1,0:T(1,128)}, f32[1,4096]{1,0:T(1,128)S(1)}, u32[]{:S(2)}, u32[]{:S(2)}) collective-permute-start(f32[1,4096]{1,0:T(1,128)} %param.13), channel_id=1, source_target_pairs={{0,2},{1,3},{2,4},{3,5},{4,6},{5,7},{6,0},{7,1},{8,10},{9,11},{10,... | collective-permute-start | bytes 49160 | tf_op jit(solution)/shard_map/ppermute | solution.py:13
  8.8 15.4 %collective-permute-start.2 = (f32[1,4096]{1,0:T(1,128)}, f32[1,4096]{1,0:T(1,128)S(1)}, u32[]{:S(2)}, u32[]{:S(2)}) collective-permute-start(f32[1,4096]{1,0:T(1,128)} %param.13), channel_id=1, source_target_pairs={{0,3},{1,4},{2,5},{3,6},{4,7},{5,0},{6,1},{7,2},{8,11},{9,12},{10,... | collective-permute-start | bytes 49160 | tf_op jit(solution)/shard_map/ppermute | solution.py:13
  14.1 10.0 %collective-permute-start.3 = (f32[1,4096]{1,0:T(1,128)}, f32[1,4096]{1,0:T(1,128)S(1)}, u32[]{:S(2)}, u32[]{:S(2)}) collective-permute-start(f32[1,4096]{1,0:T(1,128)} %param.13), channel_id=1, source_target_pairs={{0,4},{1,5},{2,6},{3,7},{4,0},{5,1},{6,2},{7,3},{8,12},{9,13},{10,... | collective-permute-start | bytes 49160 | tf_op jit(solution)/shard_map/ppermute | solution.py:13
  53.9 8.4 %collective-permute-start.14 = (f32[1,4096]{1,0:T(1,128)S(1)}, f32[1,4096]{1,0:T(1,128)S(1)}, u32[]{:S(2)}, u32[]{:S(2)}) collective-permute-start(f32[1,4096]{1,0:T(1,128)S(1)} %get-tuple-element.69), channel_id=1, source_target_pairs={{0,1},{1,2},{2,3},{3,4},{4,5},{5,6},{6,7},{7,0},{8,9},{9,10},{10,1... | collective-permute-start | bytes 49160 | tf_op jit(solution)/shard_map/ppermute | solution.py:13
  56.1 9.7 %collective-permute-start.16 = (f32[1,4096]{1,0:T(1,128)S(1)}, f32[1,4096]{1,0:T(1,128)S(1)}, u32[]{:S(2)}, u32[]{:S(2)}) collective-permute-start(f32[1,4096]{1,0:T(1,128)S(1)} %get-tuple-element.69), channel_id=1, source_target_pairs={{0,3},{1,4},{2,5},{3,6},{4,7},{5,0},{6,1},{7,2},{8,11},{9,12},{10,... | collective-permute-start | bytes 49160 | tf_op jit(solution)/shard_map/ppermute | solution.py:13
  75.0 10.0 %collective-permute-start.21 = (f32[1,4096]{1,0:T(1,128)S(1)}, f32[1,4096]{1,0:T(1,128)S(1)}, u32[]{:S(2)}, u32[]{:S(2)}) collective-permute-start(f32[1,4096]{1,0:T(1,128)S(1)} %get-tuple-element.67), channel_id=1, source_target_pairs={{0,1},{1,2},{2,3},{3,4},{4,5},{5,6},{6,7},{7,0},{8,9},{9,10},{10,1... | collective-permute-start | bytes 49160 | tf_op jit(solution)/shard_map/ppermute | solution.py:13
  76.3 8.7 %collective-permute-start.22 = (f32[1,4096]{1,0:T(1,128)S(1)}, f32[1,4096]{1,0:T(1,128)S(1)}, u32[]{:S(2)}, u32[]{:S(2)}) collective-permute-start(f32[1,4096]{1,0:T(1,128)S(1)} %get-tuple-element.67), channel_id=1, source_target_pairs={{0,2},{1,3},{2,4},{3,5},{4,6},{5,7},{6,0},{7,1},{8,10},{9,11},{10,... | collective-permute-start | bytes 49160 | tf_op jit(solution)/shard_map/ppermute | solution.py:13
  96.5 9.1 %collective-permute-start.28 = (f32[1,4096]{1,0:T(1,128)S(1)}, f32[1,4096]{1,0:T(1,128)S(1)}, u32[]{:S(2)}, u32[]{:S(2)}) collective-permute-start(f32[1,4096]{1,0:T(1,128)S(1)} %get-tuple-element.65), channel_id=1, source_target_pairs={{0,1},{1,2},{2,3},{3,4},{4,5},{5,6},{6,7},{7,0},{8,9},{9,10},{10,1... | collective-permute-start | bytes 49160 | tf_op jit(solution)/shard_map/ppermute | solution.py:13
  99.5 8.4 %collective-permute-start.30 = (f32[1,4096]{1,0:T(1,128)S(1)}, f32[1,4096]{1,0:T(1,128)S(1)}, u32[]{:S(2)}, u32[]{:S(2)}) collective-permute-start(f32[1,4096]{1,0:T(1,128)S(1)} %get-tuple-element.65), channel_id=1, source_target_pairs={{0,3},{1,4},{2,5},{3,6},{4,7},{5,0},{6,1},{7,2},{8,11},{9,12},{10,... | collective-permute-start | bytes 49160 | tf_op jit(solution)/shard_map/ppermute | solution.py:13
  117.8 9.4 %collective-permute-start.35 = (f32[1,4096]{1,0:T(1,128)S(1)}, f32[1,4096]{1,0:T(1,128)S(1)}, u32[]{:S(2)}, u32[]{:S(2)}) collective-permute-start(f32[1,4096]{1,0:T(1,128)S(1)} %get-tuple-element.63), channel_id=1, source_target_pairs={{0,1},{1,2},{2,3},{3,4},{4,5},{5,6},{6,7},{7,0},{8,9},{9,10},{10,1... | collective-permute-start | bytes 49160 | tf_op jit(solution)/shard_map/ppermute | solution.py:13
  119.3 8.8 %collective-permute-start.36 = (f32[1,4096]{1,0:T(1,128)S(1)}, f32[1,4096]{1,0:T(1,128)S(1)}, u32[]{:S(2)}, u32[]{:S(2)}) collective-permute-start(f32[1,4096]{1,0:T(1,128)S(1)} %get-tuple-element.63), channel_id=1, source_target_pairs={{0,2},{1,3},{2,4},{3,5},{4,6},{5,7},{6,0},{7,1},{8,10},{9,11},{10,... | collective-permute-start | bytes 49160 | tf_op jit(solution)/shard_map/ppermute | solution.py:13
  139.6 8.8 %collective-permute-start.42 = (f32[1,4096]{1,0:T(1,128)S(1)}, f32[1,4096]{1,0:T(1,128)S(1)}, u32[]{:S(2)}, u32[]{:S(2)}) collective-permute-start(f32[1,4096]{1,0:T(1,128)S(1)} %get-tuple-element.61), channel_id=1, source_target_pairs={{0,1},{1,2},{2,3},{3,4},{4,5},{5,6},{6,7},{7,0},{8,9},{9,10},{10,1... | collective-permute-start | bytes 49160 | tf_op jit(solution)/shard_map/ppermute | solution.py:13
  142.1 8.4 %collective-permute-start.44 = (f32[1,4096]{1,0:T(1,128)S(1)}, f32[1,4096]{1,0:T(1,128)S(1)}, u32[]{:S(2)}, u32[]{:S(2)}) collective-permute-start(f32[1,4096]{1,0:T(1,128)S(1)} %get-tuple-element.61), channel_id=1, source_target_pairs={{0,3},{1,4},{2,5},{3,6},{4,7},{5,0},{6,1},{7,2},{8,11},{9,12},{10,... | collective-permute-start | bytes 49160 | tf_op jit(solution)/shard_map/ppermute | solution.py:13
  160.5 9.1 %collective-permute-start.49 = (f32[1,4096]{1,0:T(1,128)S(1)}, f32[1,4096]{1,0:T(1,128)S(1)}, u32[]{:S(2)}, u32[]{:S(2)}) collective-permute-start(f32[1,4096]{1,0:T(1,128)S(1)} %get-tuple-element.59), channel_id=1, source_target_pairs={{0,1},{1,2},{2,3},{3,4},{4,5},{5,6},{6,7},{7,0},{8,9},{9,10},{10,1... | collective-permute-start | bytes 49160 | tf_op jit(solution)/shard_map/ppermute | solution.py:13
  182.0 8.9 %collective-permute-start.56 = (f32[1,4096]{1,0:T(1,128)S(1)}, f32[1,4096]{1,0:T(1,128)S(1)}, u32[]{:S(2)}, u32[]{:S(2)}) collective-permute-start(f32[1,4096]{1,0:T(1,128)S(1)} %get-tuple-element.55), channel_id=1, source_target_pairs={{0,1},{1,2},{2,3},{3,4},{4,5},{5,6},{6,7},{7,0},{8,9},{9,10},{10,1... | collective-permute-start | bytes 49160 | tf_op jit(solution)/shard_map/ppermute | solution.py:13
  182.8 8.7 %collective-permute-start.57 = (f32[1,4096]{1,0:T(1,128)S(1)}, f32[1,4096]{1,0:T(1,128)S(1)}, u32[]{:S(2)}, u32[]{:S(2)}) collective-permute-start(f32[1,4096]{1,0:T(1,128)S(1)} %get-tuple-element.55), channel_id=1, source_target_pairs={{0,2},{1,3},{2,4},{3,5},{4,6},{5,7},{6,0},{7,1},{8,10},{9,11},{10,... | collective-permute-start | bytes 49160 | tf_op jit(solution)/shard_map/ppermute | solution.py:13
  184.7 8.4 %collective-permute-start.58 = (f32[1,4096]{1,0:T(1,128)S(1)}, f32[1,4096]{1,0:T(1,128)S(1)}, u32[]{:S(2)}, u32[]{:S(2)}) collective-permute-start(f32[1,4096]{1,0:T(1,128)S(1)} %get-tuple-element.55), channel_id=1, source_target_pairs={{0,3},{1,4},{2,5},{3,6},{4,7},{5,0},{6,1},{7,2},{8,11},{9,12},{10,... | collective-permute-start | bytes 49160 | tf_op jit(solution)/shard_map/ppermute | solution.py:13
  209.2 9.2 %collective-permute-start.65 = (f32[1,4096]{1,0:T(1,128)S(1)}, f32[1,4096]{1,0:T(1,128)S(1)}, u32[]{:S(2)}, u32[]{:S(2)}) collective-permute-start(f32[1,4096]{1,0:T(1,128)S(1)} %get-tuple-element.53), channel_id=1, source_target_pairs={{0,1},{1,2},{2,3},{3,4},{4,5},{5,6},{6,7},{7,0},{8,9},{9,10},{10,1... | collective-permute-start | bytes 49160 | tf_op jit(solution)/shard_map/ppermute | solution.py:13
  230.4 9.0 %collective-permute-start.72 = (f32[1,4096]{1,0:T(1,128)S(1)}, f32[1,4096]{1,0:T(1,128)S(1)}, u32[]{:S(2)}, u32[]{:S(2)}) collective-permute-start(f32[1,4096]{1,0:T(1,128)S(1)} %get-tuple-element.51), channel_id=1, source_target_pairs={{0,1},{1,2},{2,3},{3,4},{4,5},{5,6},{6,7},{7,0},{8,9},{9,10},{10,1... | collective-permute-start | bytes 49160 | tf_op jit(solution)/shard_map/ppermute | solution.py:13
  231.8 8.4 %collective-permute-start.73 = (f32[1,4096]{1,0:T(1,128)S(1)}, f32[1,4096]{1,0:T(1,128)S(1)}, u32[]{:S(2)}, u32[]{:S(2)}) collective-permute-start(f32[1,4096]{1,0:T(1,128)S(1)} %get-tuple-element.51), channel_id=1, source_target_pairs={{0,2},{1,3},{2,4},{3,5},{4,6},{5,7},{6,0},{7,1},{8,10},{9,11},{10,... | collective-permute-start | bytes 49160 | tf_op jit(solution)/shard_map/ppermute | solution.py:13
  251.9 9.0 %collective-permute-start.79 = (f32[1,4096]{1,0:T(1,128)S(1)}, f32[1,4096]{1,0:T(1,128)S(1)}, u32[]{:S(2)}, u32[]{:S(2)}) collective-permute-start(f32[1,4096]{1,0:T(1,128)S(1)} %get-tuple-element.49), channel_id=1, source_target_pairs={{0,1},{1,2},{2,3},{3,4},{4,5},{5,6},{6,7},{7,0},{8,9},{9,10},{10,1... | collective-permute-start | bytes 49160 | tf_op jit(solution)/shard_map/ppermute | solution.py:13
  253.1 8.8 %collective-permute-start.80 = (f32[1,4096]{1,0:T(1,128)S(1)}, f32[1,4096]{1,0:T(1,128)S(1)}, u32[]{:S(2)}, u32[]{:S(2)}) collective-permute-start(f32[1,4096]{1,0:T(1,128)S(1)} %get-tuple-element.49), channel_id=1, source_target_pairs={{0,2},{1,3},{2,4},{3,5},{4,6},{5,7},{6,0},{7,1},{8,10},{9,11},{10,... | collective-permute-start | bytes 49160 | tf_op jit(solution)/shard_map/ppermute | solution.py:13
  273.5 8.8 %collective-permute-start.86 = (f32[1,4096]{1,0:T(1,128)S(1)}, f32[1,4096]{1,0:T(1,128)S(1)}, u32[]{:S(2)}, u32[]{:S(2)}) collective-permute-start(f32[1,4096]{1,0:T(1,128)S(1)} %get-tuple-element.47), channel_id=1, source_target_pairs={{0,1},{1,2},{2,3},{3,4},{4,5},{5,6},{6,7},{7,0},{8,9},{9,10},{10,1... | collective-permute-start | bytes 49160 | tf_op jit(solution)/shard_map/ppermute | solution.py:13
  274.3 8.5 %collective-permute-start.87 = (f32[1,4096]{1,0:T(1,128)S(1)}, f32[1,4096]{1,0:T(1,128)S(1)}, u32[]{:S(2)}, u32[]{:S(2)}) collective-permute-start(f32[1,4096]{1,0:T(1,128)S(1)} %get-tuple-element.47), channel_id=1, source_target_pairs={{0,2},{1,3},{2,4},{3,5},{4,6},{5,7},{6,0},{7,1},{8,10},{9,11},{10,... | collective-permute-start | bytes 49160 | tf_op jit(solution)/shard_map/ppermute | solution.py:13
  294.6 9.0 %collective-permute-start.93 = (f32[1,4096]{1,0:T(1,128)S(1)}, f32[1,4096]{1,0:T(1,128)S(1)}, u32[]{:S(2)}, u32[]{:S(2)}) collective-permute-start(f32[1,4096]{1,0:T(1,128)S(1)} %get-tuple-element.45), channel_id=1, source_target_pairs={{0,1},{1,2},{2,3},{3,4},{4,5},{5,6},{6,7},{7,0},{8,9},{9,10},{10,1... | collective-permute-start | bytes 49160 | tf_op jit(solution)/shard_map/ppermute | solution.py:13
  316.0 9.0 %collective-permute-start.100 = (f32[1,4096]{1,0:T(1,128)S(1)}, f32[1,4096]{1,0:T(1,128)S(1)}, u32[]{:S(2)}, u32[]{:S(2)}) collective-permute-start(f32[1,4096]{1,0:T(1,128)S(1)} %get-tuple-element.43), channel_id=1, source_target_pairs={{0,1},{1,2},{2,3},{3,4},{4,5},{5,6},{6,7},{7,0},{8,9},{9,10},{10,1... | collective-permute-start | bytes 49160 | tf_op jit(solution)/shard_map/ppermute | solution.py:13
  317.0 8.7 %collective-permute-start.101 = (f32[1,4096]{1,0:T(1,128)S(1)}, f32[1,4096]{1,0:T(1,128)S(1)}, u32[]{:S(2)}, u32[]{:S(2)}) collective-permute-start(f32[1,4096]{1,0:T(1,128)S(1)} %get-tuple-element.43), channel_id=1, source_target_pairs={{0,2},{1,3},{2,4},{3,5},{4,6},{5,7},{6,0},{7,1},{8,10},{9,11},{10,... | collective-permute-start | bytes 49160 | tf_op jit(solution)/shard_map/ppermute | solution.py:13
  318.9 8.5 %collective-permute-start.102 = (f32[1,4096]{1,0:T(1,128)S(1)}, f32[1,4096]{1,0:T(1,128)S(1)}, u32[]{:S(2)}, u32[]{:S(2)}) collective-permute-start(f32[1,4096]{1,0:T(1,128)S(1)} %get-tuple-element.43), channel_id=1, source_target_pairs={{0,3},{1,4},{2,5},{3,6},{4,7},{5,0},{6,1},{7,2},{8,11},{9,12},{10,... | collective-permute-start | bytes 49160 | tf_op jit(solution)/shard_map/ppermute | solution.py:13
  337.5 9.2 %collective-permute-start.107 = (f32[1,4096]{1,0:T(1,128)S(1)}, f32[1,4096]{1,0:T(1,128)S(1)}, u32[]{:S(2)}, u32[]{:S(2)}) collective-permute-start(f32[1,4096]{1,0:T(1,128)S(1)} %get-tuple-element.41), channel_id=1, source_target_pairs={{0,1},{1,2},{2,3},{3,4},{4,5},{5,6},{6,7},{7,0},{8,9},{9,10},{10,1... | collective-permute-start | bytes 49160 | tf_op jit(solution)/shard_map/ppermute | solution.py:13
  338.6 8.5 %collective-permute-start.108 = (f32[1,4096]{1,0:T(1,128)S(1)}, f32[1,4096]{1,0:T(1,128)S(1)}, u32[]{:S(2)}, u32[]{:S(2)}) collective-permute-start(f32[1,4096]{1,0:T(1,128)S(1)} %get-tuple-element.41), channel_id=1, source_target_pairs={{0,2},{1,3},{2,4},{3,5},{4,6},{5,7},{6,0},{7,1},{8,10},{9,11},{10,... | collective-permute-start | bytes 49160 | tf_op jit(solution)/shard_map/ppermute | solution.py:13
  358.7 9.1 %collective-permute-start.114 = (f32[1,4096]{1,0:T(1,128)S(1)}, f32[1,4096]{1,0:T(1,128)S(1)}, u32[]{:S(2)}, u32[]{:S(2)}) collective-permute-start(f32[1,4096]{1,0:T(1,128)S(1)} %get-tuple-element.37), channel_id=1, source_target_pairs={{0,1},{1,2},{2,3},{3,4},{4,5},{5,6},{6,7},{7,0},{8,9},{9,10},{10,1... | collective-permute-start | bytes 49160 | tf_op jit(solution)/shard_map/ppermute | solution.py:13
  385.2 8.9 %collective-permute-start.123 = (f32[1,4096]{1,0:T(1,128)S(1)}, f32[1,4096]{1,0:T(1,128)S(1)}, u32[]{:S(2)}, u32[]{:S(2)}) collective-permute-start(f32[1,4096]{1,0:T(1,128)S(1)} %get-tuple-element.35), channel_id=1, source_target_pairs={{0,1},{1,2},{2,3},{3,4},{4,5},{5,6},{6,7},{7,0},{8,9},{9,10},{10,1... | collective-permute-start | bytes 49160 | tf_op jit(solution)/shard_map/ppermute | solution.py:13
  386.2 8.8 %collective-permute-start.124 = (f32[1,4096]{1,0:T(1,128)S(1)}, f32[1,4096]{1,0:T(1,128)S(1)}, u32[]{:S(2)}, u32[]{:S(2)}) collective-permute-start(f32[1,4096]{1,0:T(1,128)S(1)} %get-tuple-element.35), channel_id=1, source_target_pairs={{0,2},{1,3},{2,4},{3,5},{4,6},{5,7},{6,0},{7,1},{8,10},{9,11},{10,... | collective-permute-start | bytes 49160 | tf_op jit(solution)/shard_map/ppermute | solution.py:13
  406.6 8.9 %collective-permute-start.130 = (f32[1,4096]{1,0:T(1,128)S(1)}, f32[1,4096]{1,0:T(1,128)S(1)}, u32[]{:S(2)}, u32[]{:S(2)}) collective-permute-start(f32[1,4096]{1,0:T(1,128)S(1)} %get-tuple-element.33), channel_id=1, source_target_pairs={{0,1},{1,2},{2,3},{3,4},{4,5},{5,6},{6,7},{7,0},{8,9},{9,10},{10,1... | collective-permute-start | bytes 49160 | tf_op jit(solution)/shard_map/ppermute | solution.py:13
  407.5 8.6 %collective-permute-start.131 = (f32[1,4096]{1,0:T(1,128)S(1)}, f32[1,4096]{1,0:T(1,128)S(1)}, u32[]{:S(2)}, u32[]{:S(2)}) collective-permute-start(f32[1,4096]{1,0:T(1,128)S(1)} %get-tuple-element.33), channel_id=1, source_target_pairs={{0,2},{1,3},{2,4},{3,5},{4,6},{5,7},{6,0},{7,1},{8,10},{9,11},{10,... | collective-permute-start | bytes 49160 | tf_op jit(solution)/shard_map/ppermute | solution.py:13
  427.8 8.9 %collective-permute-start.137 = (f32[1,4096]{1,0:T(1,128)S(1)}, f32[1,4096]{1,0:T(1,128)S(1)}, u32[]{:S(2)}, u32[]{:S(2)}) collective-permute-start(f32[1,4096]{1,0:T(1,128)S(1)} %get-tuple-element.31), channel_id=1, source_target_pairs={{0,1},{1,2},{2,3},{3,4},{4,5},{5,6},{6,7},{7,0},{8,9},{9,10},{10,1... | collective-permute-start | bytes 49160 | tf_op jit(solution)/shard_map/ppermute | solution.py:13
  449.0 9.1 %collective-permute-start.144 = (f32[1,4096]{1,0:T(1,128)S(1)}, f32[1,4096]{1,0:T(1,128)S(1)}, u32[]{:S(2)}, u32[]{:S(2)}) collective-permute-start(f32[1,4096]{1,0:T(1,128)S(1)} %get-tuple-element.29), channel_id=1, source_target_pairs={{0,1},{1,2},{2,3},{3,4},{4,5},{5,6},{6,7},{7,0},{8,9},{9,10},{10,1... | collective-permute-start | bytes 49160 | tf_op jit(solution)/shard_map/ppermute | solution.py:13
  450.1 8.7 %collective-permute-start.145 = (f32[1,4096]{1,0:T(1,128)S(1)}, f32[1,4096]{1,0:T(1,128)S(1)}, u32[]{:S(2)}, u32[]{:S(2)}) collective-permute-start(f32[1,4096]{1,0:T(1,128)S(1)} %get-tuple-element.29), channel_id=1, source_target_pairs={{0,2},{1,3},{2,4},{3,5},{4,6},{5,7},{6,0},{7,1},{8,10},{9,11},{10,... | collective-permute-start | bytes 49160 | tf_op jit(solution)/shard_map/ppermute | solution.py:13
  470.7 9.0 %collective-permute-start.151 = (f32[1,4096]{1,0:T(1,128)S(1)}, f32[1,4096]{1,0:T(1,128)S(1)}, u32[]{:S(2)}, u32[]{:S(2)}) collective-permute-start(f32[1,4096]{1,0:T(1,128)S(1)} %get-tuple-element.27), channel_id=1, source_target_pairs={{0,1},{1,2},{2,3},{3,4},{4,5},{5,6},{6,7},{7,0},{8,9},{9,10},{10,1... | collective-permute-start | bytes 49160 | tf_op jit(solution)/shard_map/ppermute | solution.py:13
  471.5 8.6 %collective-permute-start.152 = (f32[1,4096]{1,0:T(1,128)S(1)}, f32[1,4096]{1,0:T(1,128)S(1)}, u32[]{:S(2)}, u32[]{:S(2)}) collective-permute-start(f32[1,4096]{1,0:T(1,128)S(1)} %get-tuple-element.27), channel_id=1, source_target_pairs={{0,2},{1,3},{2,4},{3,5},{4,6},{5,7},{6,0},{7,1},{8,10},{9,11},{10,... | collective-permute-start | bytes 49160 | tf_op jit(solution)/shard_map/ppermute | solution.py:13
  491.7 9.0 %collective-permute-start.158 = (f32[1,4096]{1,0:T(1,128)S(1)}, f32[1,4096]{1,0:T(1,128)S(1)}, u32[]{:S(2)}, u32[]{:S(2)}) collective-permute-start(f32[1,4096]{1,0:T(1,128)S(1)} %get-tuple-element.25), channel_id=1, source_target_pairs={{0,1},{1,2},{2,3},{3,4},{4,5},{5,6},{6,7},{7,0},{8,9},{9,10},{10,1... | collective-permute-start | bytes 49160 | tf_op jit(solution)/shard_map/ppermute | solution.py:13
  493.0 8.5 %collective-permute-start.159 = (f32[1,4096]{1,0:T(1,128)S(1)}, f32[1,4096]{1,0:T(1,128)S(1)}, u32[]{:S(2)}, u32[]{:S(2)}) collective-permute-start(f32[1,4096]{1,0:T(1,128)S(1)} %get-tuple-element.25), channel_id=1, source_target_pairs={{0,2},{1,3},{2,4},{3,5},{4,6},{5,7},{6,0},{7,1},{8,10},{9,11},{10,... | collective-permute-start | bytes 49160 | tf_op jit(solution)/shard_map/ppermute | solution.py:13
  513.3 8.9 %collective-permute-start.165 = (f32[1,4096]{1,0:T(1,128)S(1)}, f32[1,4096]{1,0:T(1,128)S(1)}, u32[]{:S(2)}, u32[]{:S(2)}) collective-permute-start(f32[1,4096]{1,0:T(1,128)S(1)} %get-tuple-element.23), channel_id=1, source_target_pairs={{0,1},{1,2},{2,3},{3,4},{4,5},{5,6},{6,7},{7,0},{8,9},{9,10},{10,1... | collective-permute-start | bytes 49160 | tf_op jit(solution)/shard_map/ppermute | solution.py:13
  514.4 8.8 %collective-permute-start.166 = (f32[1,4096]{1,0:T(1,128)S(1)}, f32[1,4096]{1,0:T(1,128)S(1)}, u32[]{:S(2)}, u32[]{:S(2)}) collective-permute-start(f32[1,4096]{1,0:T(1,128)S(1)} %get-tuple-element.23), channel_id=1, source_target_pairs={{0,2},{1,3},{2,4},{3,5},{4,6},{5,7},{6,0},{7,1},{8,10},{9,11},{10,... | collective-permute-start | bytes 49160 | tf_op jit(solution)/shard_map/ppermute | solution.py:13
  516.3 8.4 %collective-permute-start.167 = (f32[1,4096]{1,0:T(1,128)S(1)}, f32[1,4096]{1,0:T(1,128)S(1)}, u32[]{:S(2)}, u32[]{:S(2)}) collective-permute-start(f32[1,4096]{1,0:T(1,128)S(1)} %get-tuple-element.23), channel_id=1, source_target_pairs={{0,3},{1,4},{2,5},{3,6},{4,7},{5,0},{6,1},{7,2},{8,11},{9,12},{10,... | collective-permute-start | bytes 49160 | tf_op jit(solution)/shard_map/ppermute | solution.py:13
  534.8 9.0 %collective-permute-start.172 = (f32[1,4096]{1,0:T(1,128)S(1)}, f32[1,4096]{1,0:T(1,128)S(1)}, u32[]{:S(2)}, u32[]{:S(2)}) collective-permute-start(f32[1,4096]{1,0:T(1,128)S(1)} %get-tuple-element.19), channel_id=1, source_target_pairs={{0,1},{1,2},{2,3},{3,4},{4,5},{5,6},{6,7},{7,0},{8,9},{9,10},{10,1... | collective-permute-start | bytes 49160 | tf_op jit(solution)/shard_map/ppermute | solution.py:13
  535.8 8.4 %collective-permute-start.173 = (f32[1,4096]{1,0:T(1,128)S(1)}, f32[1,4096]{1,0:T(1,128)S(1)}, u32[]{:S(2)}, u32[]{:S(2)}) collective-permute-start(f32[1,4096]{1,0:T(1,128)S(1)} %get-tuple-element.19), channel_id=1, source_target_pairs={{0,2},{1,3},{2,4},{3,5},{4,6},{5,7},{6,0},{7,1},{8,10},{9,11},{10,... | collective-permute-start | bytes 49160 | tf_op jit(solution)/shard_map/ppermute | solution.py:13
  561.9 8.9 %collective-permute-start.181 = (f32[1,4096]{1,0:T(1,128)S(1)}, f32[1,4096]{1,0:T(1,128)S(1)}, u32[]{:S(2)}, u32[]{:S(2)}) collective-permute-start(f32[1,4096]{1,0:T(1,128)S(1)} %get-tuple-element.17), channel_id=1, source_target_pairs={{0,1},{1,2},{2,3},{3,4},{4,5},{5,6},{6,7},{7,0},{8,9},{9,10},{10,1... | collective-permute-start | bytes 49160 | tf_op jit(solution)/shard_map/ppermute | solution.py:13
  583.0 9.1 %collective-permute-start.188 = (f32[1,4096]{1,0:T(1,128)S(1)}, f32[1,4096]{1,0:T(1,128)S(1)}, u32[]{:S(2)}, u32[]{:S(2)}) collective-permute-start(f32[1,4096]{1,0:T(1,128)S(1)} %get-tuple-element.15), channel_id=1, source_target_pairs={{0,1},{1,2},{2,3},{3,4},{4,5},{5,6},{6,7},{7,0},{8,9},{9,10},{10,1... | collective-permute-start | bytes 49160 | tf_op jit(solution)/shard_map/ppermute | solution.py:13
  584.2 8.8 %collective-permute-start.189 = (f32[1,4096]{1,0:T(1,128)S(1)}, f32[1,4096]{1,0:T(1,128)S(1)}, u32[]{:S(2)}, u32[]{:S(2)}) collective-permute-start(f32[1,4096]{1,0:T(1,128)S(1)} %get-tuple-element.15), channel_id=1, source_target_pairs={{0,2},{1,3},{2,4},{3,5},{4,6},{5,7},{6,0},{7,1},{8,10},{9,11},{10,... | collective-permute-start | bytes 49160 | tf_op jit(solution)/shard_map/ppermute | solution.py:13
  604.6 8.8 %collective-permute-start.195 = (f32[1,4096]{1,0:T(1,128)S(1)}, f32[1,4096]{1,0:T(1,128)S(1)}, u32[]{:S(2)}, u32[]{:S(2)}) collective-permute-start(f32[1,4096]{1,0:T(1,128)S(1)} %get-tuple-element.13), channel_id=1, source_target_pairs={{0,1},{1,2},{2,3},{3,4},{4,5},{5,6},{6,7},{7,0},{8,9},{9,10},{10,1... | collective-permute-start | bytes 49160 | tf_op jit(solution)/shard_map/ppermute | solution.py:13
  605.4 8.6 %collective-permute-start.196 = (f32[1,4096]{1,0:T(1,128)S(1)}, f32[1,4096]{1,0:T(1,128)S(1)}, u32[]{:S(2)}, u32[]{:S(2)}) collective-permute-start(f32[1,4096]{1,0:T(1,128)S(1)} %get-tuple-element.13), channel_id=1, source_target_pairs={{0,2},{1,3},{2,4},{3,5},{4,6},{5,7},{6,0},{7,1},{8,10},{9,11},{10,... | collective-permute-start | bytes 49160 | tf_op jit(solution)/shard_map/ppermute | solution.py:13
  625.4 9.0 %collective-permute-start.202 = (f32[1,4096]{1,0:T(1,128)S(1)}, f32[1,4096]{1,0:T(1,128)S(1)}, u32[]{:S(2)}, u32[]{:S(2)}) collective-permute-start(f32[1,4096]{1,0:T(1,128)S(1)} %get-tuple-element.11), channel_id=1, source_target_pairs={{0,1},{1,2},{2,3},{3,4},{4,5},{5,6},{6,7},{7,0},{8,9},{9,10},{10,1... | collective-permute-start | bytes 49160 | tf_op jit(solution)/shard_map/ppermute | solution.py:13
  646.8 9.1 %collective-permute-start.209 = (f32[1,4096]{1,0:T(1,128)S(1)}, f32[1,4096]{1,0:T(1,128)S(1)}, u32[]{:S(2)}, u32[]{:S(2)}) collective-permute-start(f32[1,4096]{1,0:T(1,128)S(1)} %get-tuple-element.9), channel_id=1, source_target_pairs={{0,1},{1,2},{2,3},{3,4},{4,5},{5,6},{6,7},{7,0},{8,9},{9,10},{10,1... | collective-permute-start | bytes 49160 | tf_op jit(solution)/shard_map/ppermute | solution.py:13
  647.9 8.6 %collective-permute-start.210 = (f32[1,4096]{1,0:T(1,128)S(1)}, f32[1,4096]{1,0:T(1,128)S(1)}, u32[]{:S(2)}, u32[]{:S(2)}) collective-permute-start(f32[1,4096]{1,0:T(1,128)S(1)} %get-tuple-element.9), channel_id=1, source_target_pairs={{0,2},{1,3},{2,4},{3,5},{4,6},{5,7},{6,0},{7,1},{8,10},{9,11},{10,... | collective-permute-start | bytes 49160 | tf_op jit(solution)/shard_map/ppermute | solution.py:13
  668.0 9.0 %collective-permute-start.216 = (f32[1,4096]{1,0:T(1,128)S(1)}, f32[1,4096]{1,0:T(1,128)S(1)}, u32[]{:S(2)}, u32[]{:S(2)}) collective-permute-start(f32[1,4096]{1,0:T(1,128)S(1)} %get-tuple-element.7), channel_id=1, source_target_pairs={{0,1},{1,2},{2,3},{3,4},{4,5},{5,6},{6,7},{7,0},{8,9},{9,10},{10,1... | collective-permute-start | bytes 49160 | tf_op jit(solution)/shard_map/ppermute | solution.py:13
  669.1 8.5 %collective-permute-start.217 = (f32[1,4096]{1,0:T(1,128)S(1)}, f32[1,4096]{1,0:T(1,128)S(1)}, u32[]{:S(2)}, u32[]{:S(2)}) collective-permute-start(f32[1,4096]{1,0:T(1,128)S(1)} %get-tuple-element.7), channel_id=1, source_target_pairs={{0,2},{1,3},{2,4},{3,5},{4,6},{5,7},{6,0},{7,1},{8,10},{9,11},{10,... | collective-permute-start | bytes 49160 | tf_op jit(solution)/shard_map/ppermute | solution.py:13
  689.3 9.2 %collective-permute-start.223 = (f32[1,4096]{1,0:T(1,128)S(1)}, f32[1,4096]{1,0:T(1,128)S(1)}, u32[]{:S(2)}, u32[]{:S(2)}) collective-permute-start(f32[1,4096]{1,0:T(1,128)S(1)} %get-tuple-element.5), channel_id=1, source_target_pairs={{0,1},{1,2},{2,3},{3,4},{4,5},{5,6},{6,7},{7,0},{8,9},{9,10},{10,1... | collective-permute-start | bytes 49160 | tf_op jit(solution)/shard_map/ppermute | solution.py:13
  690.5 8.8 %collective-permute-start.224 = (f32[1,4096]{1,0:T(1,128)S(1)}, f32[1,4096]{1,0:T(1,128)S(1)}, u32[]{:S(2)}, u32[]{:S(2)}) collective-permute-start(f32[1,4096]{1,0:T(1,128)S(1)} %get-tuple-element.5), channel_id=1, source_target_pairs={{0,2},{1,3},{2,4},{3,5},{4,6},{5,7},{6,0},{7,1},{8,10},{9,11},{10,... | collective-permute-start | bytes 49160 | tf_op jit(solution)/shard_map/ppermute | solution.py:13
  711.3 8.8 %collective-permute-start.230 = (f32[1,2,64]{2,1,0:T(2,128)S(1)}, f32[1,2,64]{2,1,0:T(2,128)S(1)}, u32[]{:S(2)}, u32[]{:S(2)}) collective-permute-start(f32[1,2,64]{2,1,0:T(2,128)S(1)} %broadcast_select_fusion), channel_id=1, source_target_pairs={{0,1},{1,2},{2,3},{3,4},{4,5},{5,6},{6,7},{7,0},{8,9},{9,10},{10,1... | collective-permute-start | bytes 1544 | tf_op jit(solution)/shard_map/ppermute | solution.py:13
  712.1 8.7 %collective-permute-start.231 = (f32[1,2,64]{2,1,0:T(2,128)S(1)}, f32[1,2,64]{2,1,0:T(2,128)S(1)}, u32[]{:S(2)}, u32[]{:S(2)}) collective-permute-start(f32[1,2,64]{2,1,0:T(2,128)S(1)} %broadcast_select_fusion), channel_id=1, source_target_pairs={{0,2},{1,3},{2,4},{3,5},{4,6},{5,7},{6,0},{7,1},{8,10},{9,11},{10,... | collective-permute-start | bytes 1544 | tf_op jit(solution)/shard_map/ppermute | solution.py:13
  (185 other events, 1344.2 us)

commit v2 on v1

--- a/solution.py
+++ b/solution.py
@@ -15,14 +15,8 @@
 
 def collect(value):
     count = lax.axis_size("sub")
-    parts = [value] + [shifted(value, "sub", k) for k in range(1, count)]
-    return jnp.stack(parts)
-
-
-def rotated(index, me, count, chunk):
-    owner = index // chunk
-    slot = (me - owner) % count
-    return slot * chunk + index % chunk
+    copies = jnp.broadcast_to(value[None], (count,) + value.shape)
+    return lax.all_to_all(copies, "sub", 0, 0, tiled=True)
 
 
 def apply_blocks(blocks, own_part, others):
@@ -44,13 +38,11 @@
     width = blocks.shape[2]
     rows_here = blocks.shape[1]
     local_count = rows_here * width
-    count = lax.axis_size("sub")
-    me = lax.axis_index("sub")
-    offset = me * local_count
+    offset = lax.axis_index("sub") * local_count
     diag = jnp.diagonal(blocks[..., :width], axis1=2, axis2=3).reshape(1, local_count)
     system_diag = diag + capacity
-    remote_cols = rotated(pattern[0][:, 1:].reshape(-1), me, count, rows_here)
-    end_index = rotated(line_ends[0], me, count, local_count)
+    remote_cols = pattern[0][:, 1:].reshape(-1)
+    end_index = line_ends[0]
     local_ends = line_ends - offset
     inside = (local_ends >= 0) & (local_ends < local_count)
     safe_ends = jnp.clip(local_ends, 0, local_count - 1)

time: 740 us -> 673 us (0.909)
  starting transfers between devices: 374 us -> 122 us
  waiting for transfers between devices: 83.3 us -> 231 us
  local copies, waits for them, and re-layouts: 52.5 us -> 68.4 us
  other arithmetic: 34.3 us -> 44.8 us
  blocking collectives: 0 us -> 8.85 us
    ppermute x239 -> x8, starting transfers between devices: 374 us -> 4.74 us  [shifted(): return lax.ppermute(value, axis, pairs)]
    all_to_all x0 -> x32, waiting for transfers between devices: none -> 223 us  [collect(): return lax.all_to_all(copies, 'sub', 0, 0, tiled=True)]
    all_to_all x0 -> x32, starting transfers between devices: none -> 117 us  [collect(): return lax.all_to_all(copies, 'sub', 0, 0, tiled=True)]
    ppermute x239 -> x8, waiting for transfers between devices: 83.3 us -> 7.27 us  [shifted(): return lax.ppermute(value, axis, pairs)]
    broadcast_in_dim x0 -> x33, local copies, waits for them, and re-layouts: none -> 23.5 us  [collect(): copies = jnp.broadcast_to(value[None], (count,) + value.shape)]
    all_to_all x0 -> x33, other arithmetic: none -> 10.5 us  [collect(): return lax.all_to_all(copies, 'sub', 0, 0, tiled=True)]
    all_to_all x0 -> x1, blocking collectives: none -> 8.85 us  [collect(): return lax.all_to_all(copies, 'sub', 0, 0, tiled=True)]
  transfers between devices with their start and end apart: 239 -> 40, of which waited for: 94 -> 36; matrix products, arithmetic and copies ran while one was open for 4% -> 5% of each run, Pallas kernels for 0% -> 0%
where the time goes in v2:
time: 673 us; the launch traced here: 661 us
  waiting for transfers between devices  231 us (34%)
  matrix products  183 us (27%)
  starting transfers between devices  122 us (18%)
  local copies, waits for them, and re-layouts  68.4 us (10%)
  other arithmetic  44.8 us (7%)
  blocking collectives  8.85 us (1%)
    all_to_all x32, waiting for transfers between devices, collect(): return lax.all_to_all(copies, 'sub', 0, 0, tiled=True)  223 us
    dot_general x32, matrix products, apply_blocks(): jnp.einsum('rik,rk->ri', blocks[0], picked, precision=lax.Precision.HIGHEST)  183 us
    all_to_all x32, starting transfers between devices, collect(): return lax.all_to_all(copies, 'sub', 0, 0, tiled=True)  117 us
    broadcast_in_dim x33, local copies, waits for them, and re-layouts, collect(): copies = jnp.broadcast_to(value[None], (count,) + value.shape)  23.5 us
    add x32, other arithmetic, on_device(): field = field + (rhs - result - capacity * field) / system_diag  22.3 us
    gather x32, local copies, waits for them, and re-layouts, on_device(): others = whole.reshape(-1, width)[remote_cols]  22.2 us
  transfers between devices with their start and end apart: 40, of which 36 were waited for; matrix products, arithmetic and copies ran while one was open for 5% of the time, Pallas kernels for 0%

profile of v2, /device:TPU:0, one launch (start us, length us, event | category | flops | bytes accessed | tf_op | source)
XLA Modules:
  0.0 660.6 jit_solution(6517580964072771839)
XLA Ops:
  2.2 7.3 %all-to-all-start = ((f32[8,1,4096]{2,1,0:T(1,128)}), f32[8,1,4096]{2,1,0:T(1,128)S(1)}, u32[]{:S(2)}, u32[]{:S(2)}) async-start(f32[8,1,4096]{2,1,0:T(1,128)} %broadcast_in_dim.154), calls=%async_computation | async-start | bytes 262144 | tf_op jit(solution)/shard_map/all_to_all | solution.py:19
  20.8 5.7 fusion.62
  28.1 6.0 all-to-all-start.1
  34.2 7.3 %all-to-all-done.1 = f32[8,1,4096]{2,1,0:T(1,128)S(1)} async-done(((f32[8,1,4096]{2,1,0:T(1,128)}), f32[8,1,4096]{2,1,0:T(1,128)S(1)}, u32[]{:S(2)}, u32[]{:S(2)}) %all-to-all-start.1) | async-done | bytes 131104 | tf_op jit(solution)/shard_map/all_to_all | solution.py:19
  42.7 5.7 fusion.60
  53.7 7.2 %all-to-all-done.2 = f32[8,1,4096]{2,1,0:T(1,128)S(1)} async-done(((f32[8,1,4096]{2,1,0:T(1,128)}), f32[8,1,4096]{2,1,0:T(1,128)S(1)}, u32[]{:S(2)}, u32[]{:S(2)}) %all-to-all-start.2) | async-done | bytes 131104 | tf_op jit(solution)/shard_map/all_to_all | solution.py:19
  62.1 5.7 fusion.58
  72.9 7.2 %all-to-all-done.3 = f32[8,1,4096]{2,1,0:T(1,128)S(1)} async-done(((f32[8,1,4096]{2,1,0:T(1,128)}), f32[8,1,4096]{2,1,0:T(1,128)S(1)}, u32[]{:S(2)}, u32[]{:S(2)}) %all-to-all-start.3) | async-done | bytes 131104 | tf_op jit(solution)/shard_map/all_to_all | solution.py:19
  81.3 5.7 fusion.56
  92.0 7.2 %all-to-all-done.4 = f32[8,1,4096]{2,1,0:T(1,128)S(1)} async-done(((f32[8,1,4096]{2,1,0:T(1,128)}), f32[8,1,4096]{2,1,0:T(1,128)S(1)}, u32[]{:S(2)}, u32[]{:S(2)}) %all-to-all-start.4) | async-done | bytes 131104 | tf_op jit(solution)/shard_map/all_to_all | solution.py:19
  100.5 5.7 fusion.54
  111.6 7.2 %all-to-all-done.5 = f32[8,1,4096]{2,1,0:T(1,128)S(1)} async-done(((f32[8,1,4096]{2,1,0:T(1,128)}), f32[8,1,4096]{2,1,0:T(1,128)S(1)}, u32[]{:S(2)}, u32[]{:S(2)}) %all-to-all-start.5) | async-done | bytes 131104 | tf_op jit(solution)/shard_map/all_to_all | solution.py:19
  120.1 5.7 fusion.52
  130.8 7.2 %all-to-all-done.6 = f32[8,1,4096]{2,1,0:T(1,128)S(1)} async-done(((f32[8,1,4096]{2,1,0:T(1,128)}), f32[8,1,4096]{2,1,0:T(1,128)S(1)}, u32[]{:S(2)}, u32[]{:S(2)}) %all-to-all-start.6) | async-done | bytes 131104 | tf_op jit(solution)/shard_map/all_to_all | solution.py:19
  139.3 5.7 fusion.50
  150.1 7.1 %all-to-all-done.7 = f32[8,1,4096]{2,1,0:T(1,128)S(1)} async-done(((f32[8,1,4096]{2,1,0:T(1,128)}), f32[8,1,4096]{2,1,0:T(1,128)S(1)}, u32[]{:S(2)}, u32[]{:S(2)}) %all-to-all-start.7) | async-done | bytes 131104 | tf_op jit(solution)/shard_map/all_to_all | solution.py:19
  158.5 5.7 fusion.48
  169.5 7.1 %all-to-all-done.8 = f32[8,1,4096]{2,1,0:T(1,128)S(1)} async-done(((f32[8,1,4096]{2,1,0:T(1,128)}), f32[8,1,4096]{2,1,0:T(1,128)S(1)}, u32[]{:S(2)}, u32[]{:S(2)}) %all-to-all-start.8) | async-done | bytes 131104 | tf_op jit(solution)/shard_map/all_to_all | solution.py:19
  182.1 5.7 fusion.46
  194.3 7.3 %all-to-all-done.9 = f32[8,1,4096]{2,1,0:T(1,128)S(1)} async-done(((f32[8,1,4096]{2,1,0:T(1,128)}), f32[8,1,4096]{2,1,0:T(1,128)S(1)}, u32[]{:S(2)}, u32[]{:S(2)}) %all-to-all-start.9) | async-done | bytes 131104 | tf_op jit(solution)/shard_map/all_to_all | solution.py:19
  202.9 5.7 fusion.44
  213.9 7.2 %all-to-all-done.10 = f32[8,1,4096]{2,1,0:T(1,128)S(1)} async-done(((f32[8,1,4096]{2,1,0:T(1,128)}), f32[8,1,4096]{2,1,0:T(1,128)S(1)}, u32[]{:S(2)}, u32[]{:S(2)}) %all-to-all-start.10) | async-done | bytes 131104 | tf_op jit(solution)/shard_map/all_to_all | solution.py:19
  222.3 5.7 fusion.42
  233.0 7.2 %all-to-all-done.11 = f32[8,1,4096]{2,1,0:T(1,128)S(1)} async-done(((f32[8,1,4096]{2,1,0:T(1,128)}), f32[8,1,4096]{2,1,0:T(1,128)S(1)}, u32[]{:S(2)}, u32[]{:S(2)}) %all-to-all-start.11) | async-done | bytes 131104 | tf_op jit(solution)/shard_map/all_to_all | solution.py:19
  241.5 5.7 fusion.40
  252.2 7.2 %all-to-all-done.12 = f32[8,1,4096]{2,1,0:T(1,128)S(1)} async-done(((f32[8,1,4096]{2,1,0:T(1,128)}), f32[8,1,4096]{2,1,0:T(1,128)S(1)}, u32[]{:S(2)}, u32[]{:S(2)}) %all-to-all-start.12) | async-done | bytes 131104 | tf_op jit(solution)/shard_map/all_to_all | solution.py:19
  260.7 5.7 fusion.38
  271.8 7.2 %all-to-all-done.13 = f32[8,1,4096]{2,1,0:T(1,128)S(1)} async-done(((f32[8,1,4096]{2,1,0:T(1,128)}), f32[8,1,4096]{2,1,0:T(1,128)S(1)}, u32[]{:S(2)}, u32[]{:S(2)}) %all-to-all-start.13) | async-done | bytes 131104 | tf_op jit(solution)/shard_map/all_to_all | solution.py:19
  280.3 5.7 fusion.36
  291.0 7.2 %all-to-all-done.14 = f32[8,1,4096]{2,1,0:T(1,128)S(1)} async-done(((f32[8,1,4096]{2,1,0:T(1,128)}), f32[8,1,4096]{2,1,0:T(1,128)S(1)}, u32[]{:S(2)}, u32[]{:S(2)}) %all-to-all-start.14) | async-done | bytes 131104 | tf_op jit(solution)/shard_map/all_to_all | solution.py:19
  299.5 5.7 fusion.34
  310.2 7.2 %all-to-all-done.15 = f32[8,1,4096]{2,1,0:T(1,128)S(1)} async-done(((f32[8,1,4096]{2,1,0:T(1,128)}), f32[8,1,4096]{2,1,0:T(1,128)S(1)}, u32[]{:S(2)}, u32[]{:S(2)}) %all-to-all-start.15) | async-done | bytes 131104 | tf_op jit(solution)/shard_map/all_to_all | solution.py:19
  318.7 5.7 fusion.32
  329.6 7.2 %all-to-all-done.16 = f32[8,1,4096]{2,1,0:T(1,128)S(1)} async-done(((f32[8,1,4096]{2,1,0:T(1,128)}), f32[8,1,4096]{2,1,0:T(1,128)S(1)}, u32[]{:S(2)}, u32[]{:S(2)}) %all-to-all-start.16) | async-done | bytes 131104 | tf_op jit(solution)/shard_map/all_to_all | solution.py:19
  353.5 7.3 %all-to-all-done.17 = f32[8,1,4096]{2,1,0:T(1,128)S(1)} async-done(((f32[8,1,4096]{2,1,0:T(1,128)}), f32[8,1,4096]{2,1,0:T(1,128)S(1)}, u32[]{:S(2)}, u32[]{:S(2)}) %all-to-all-start.17) | async-done | bytes 131104 | tf_op jit(solution)/shard_map/all_to_all | solution.py:19
  362.1 5.7 fusion.28
  373.0 7.2 %all-to-all-done.18 = f32[8,1,4096]{2,1,0:T(1,128)S(1)} async-done(((f32[8,1,4096]{2,1,0:T(1,128)}), f32[8,1,4096]{2,1,0:T(1,128)S(1)}, u32[]{:S(2)}, u32[]{:S(2)}) %all-to-all-start.18) | async-done | bytes 131104 | tf_op jit(solution)/shard_map/all_to_all | solution.py:19
  381.5 5.7 fusion.26
  392.2 7.2 %all-to-all-done.19 = f32[8,1,4096]{2,1,0:T(1,128)S(1)} async-done(((f32[8,1,4096]{2,1,0:T(1,128)}), f32[8,1,4096]{2,1,0:T(1,128)S(1)}, u32[]{:S(2)}, u32[]{:S(2)}) %all-to-all-start.19) | async-done | bytes 131104 | tf_op jit(solution)/shard_map/all_to_all | solution.py:19
  400.7 5.7 fusion.24
  411.4 7.2 %all-to-all-done.20 = f32[8,1,4096]{2,1,0:T(1,128)S(1)} async-done(((f32[8,1,4096]{2,1,0:T(1,128)}), f32[8,1,4096]{2,1,0:T(1,128)S(1)}, u32[]{:S(2)}, u32[]{:S(2)}) %all-to-all-start.20) | async-done | bytes 131104 | tf_op jit(solution)/shard_map/all_to_all | solution.py:19
  419.9 5.7 fusion.22
  431.0 7.2 %all-to-all-done.21 = f32[8,1,4096]{2,1,0:T(1,128)S(1)} async-done(((f32[8,1,4096]{2,1,0:T(1,128)}), f32[8,1,4096]{2,1,0:T(1,128)S(1)}, u32[]{:S(2)}, u32[]{:S(2)}) %all-to-all-start.21) | async-done | bytes 131104 | tf_op jit(solution)/shard_map/all_to_all | solution.py:19
  439.5 5.7 fusion.20
  450.2 7.2 %all-to-all-done.22 = f32[8,1,4096]{2,1,0:T(1,128)S(1)} async-done(((f32[8,1,4096]{2,1,0:T(1,128)}), f32[8,1,4096]{2,1,0:T(1,128)S(1)}, u32[]{:S(2)}, u32[]{:S(2)}) %all-to-all-start.22) | async-done | bytes 131104 | tf_op jit(solution)/shard_map/all_to_all | solution.py:19
  458.7 5.7 fusion.18
  469.4 7.2 %all-to-all-done.23 = f32[8,1,4096]{2,1,0:T(1,128)S(1)} async-done(((f32[8,1,4096]{2,1,0:T(1,128)}), f32[8,1,4096]{2,1,0:T(1,128)S(1)}, u32[]{:S(2)}, u32[]{:S(2)}) %all-to-all-start.23) | async-done | bytes 131104 | tf_op jit(solution)/shard_map/all_to_all | solution.py:19
  477.9 5.7 fusion.16
  488.8 7.2 %all-to-all-done.24 = f32[8,1,4096]{2,1,0:T(1,128)S(1)} async-done(((f32[8,1,4096]{2,1,0:T(1,128)}), f32[8,1,4096]{2,1,0:T(1,128)S(1)}, u32[]{:S(2)}, u32[]{:S(2)}) %all-to-all-start.24) | async-done | bytes 131104 | tf_op jit(solution)/shard_map/all_to_all | solution.py:19
  513.6 7.3 %all-to-all-done.25 = f32[8,1,4096]{2,1,0:T(1,128)S(1)} async-done(((f32[8,1,4096]{2,1,0:T(1,128)}), f32[8,1,4096]{2,1,0:T(1,128)S(1)}, u32[]{:S(2)}, u32[]{:S(2)}) %all-to-all-start.25) | async-done | bytes 131104 | tf_op jit(solution)/shard_map/all_to_all | solution.py:19
  522.2 5.7 fusion.12
  533.1 7.2 %all-to-all-done.26 = f32[8,1,4096]{2,1,0:T(1,128)S(1)} async-done(((f32[8,1,4096]{2,1,0:T(1,128)}), f32[8,1,4096]{2,1,0:T(1,128)S(1)}, u32[]{:S(2)}, u32[]{:S(2)}) %all-to-all-start.26) | async-done | bytes 131104 | tf_op jit(solution)/shard_map/all_to_all | solution.py:19
  541.6 5.7 fusion.10
  552.3 7.2 %all-to-all-done.27 = f32[8,1,4096]{2,1,0:T(1,128)S(1)} async-done(((f32[8,1,4096]{2,1,0:T(1,128)}), f32[8,1,4096]{2,1,0:T(1,128)S(1)}, u32[]{:S(2)}, u32[]{:S(2)}) %all-to-all-start.27) | async-done | bytes 131104 | tf_op jit(solution)/shard_map/all_to_all | solution.py:19
  560.8 5.7 fusion.8
  571.5 7.2 %all-to-all-done.28 = f32[8,1,4096]{2,1,0:T(1,128)S(1)} async-done(((f32[8,1,4096]{2,1,0:T(1,128)}), f32[8,1,4096]{2,1,0:T(1,128)S(1)}, u32[]{:S(2)}, u32[]{:S(2)}) %all-to-all-start.28) | async-done | bytes 131104 | tf_op jit(solution)/shard_map/all_to_all | solution.py:19
  580.0 5.7 fusion.6
  590.9 7.2 %all-to-all-done.29 = f32[8,1,4096]{2,1,0:T(1,128)S(1)} async-done(((f32[8,1,4096]{2,1,0:T(1,128)}), f32[8,1,4096]{2,1,0:T(1,128)S(1)}, u32[]{:S(2)}, u32[]{:S(2)}) %all-to-all-start.29) | async-done | bytes 131104 | tf_op jit(solution)/shard_map/all_to_all | solution.py:19
  599.4 5.7 fusion.4
  610.1 7.2 %all-to-all-done.30 = f32[8,1,4096]{2,1,0:T(1,128)S(1)} async-done(((f32[8,1,4096]{2,1,0:T(1,128)}), f32[8,1,4096]{2,1,0:T(1,128)S(1)}, u32[]{:S(2)}, u32[]{:S(2)}) %all-to-all-start.30) | async-done | bytes 131104 | tf_op jit(solution)/shard_map/all_to_all | solution.py:19
  618.6 5.7 fusion.2
  629.4 7.1 %all-to-all-done.31 = f32[8,1,4096]{2,1,0:T(1,128)S(1)} async-done(((f32[8,1,4096]{2,1,0:T(1,128)}), f32[8,1,4096]{2,1,0:T(1,128)S(1)}, u32[]{:S(2)}, u32[]{:S(2)}) %all-to-all-start.31) | async-done | bytes 131104 | tf_op jit(solution)/shard_map/all_to_all | solution.py:19
  637.8 5.7 fusion
  645.1 8.8 %all_to_all.165 = f32[8,1,128]{2,1,0:T(1,128)S(1)} all-to-all(f32[8,1,128]{2,1,0:T(1,128)S(1)} %reshape.1546), channel_id=1, replica_groups=mesh['area'=4,'sub'=8] {'sub'}, dimensions={0} | all-to-all | bytes 8192 | tf_op jit(solution)/shard_map/all_to_all | solution.py:19
  (415 shorter events, 240.6 us)
Async XLA Ops:
  0.6 13.5 %slice-start = ((f32[1,64,64,256]{3,2,1,0:T(8,128)}), f32[1,64,64,64]{3,2,1,0:T(8,128)S(1)}, s32[]{:S(2)}) async-start(f32[1,64,64,256]{3,2,1,0:T(8,128)} %param.8), calls=%async_computation.33 | async-start | bytes 4194304 | tf_op jit(solution)/shard_map/slice | solution.py:42
  2.2 17.3 %all-to-all-start = ((f32[8,1,4096]{2,1,0:T(1,128)}), f32[8,1,4096]{2,1,0:T(1,128)S(1)}, u32[]{:S(2)}, u32[]{:S(2)}) async-start(f32[8,1,4096]{2,1,0:T(1,128)} %broadcast_in_dim.154), calls=%async_computation | async-start | bytes 262144 | tf_op jit(solution)/shard_map/all_to_all | solution.py:19
  16.4 10.3 %copy-start.1 = (f32[1,4096]{1,0:T(1,128)S(1)}, f32[1,4096]{1,0:T(1,128)}, u32[]{:S(2)}) copy-start(f32[1,4096]{1,0:T(1,128)} %param.12) | copy-start | bytes 49156
  16.4 10.3 %copy-start.2 = (f32[1,4096]{1,0:T(1,128)S(1)}, f32[1,4096]{1,0:T(1,128)}, u32[]{:S(2)}) copy-start(f32[1,4096]{1,0:T(1,128)} %param.13) | copy-start | bytes 49156
  28.1 13.3 %all-to-all-start.1 = ((f32[8,1,4096]{2,1,0:T(1,128)}), f32[8,1,4096]{2,1,0:T(1,128)S(1)}, u32[]{:S(2)}, u32[]{:S(2)}) async-start(f32[8,1,4096]{2,1,0:T(1,128)} %broadcast_in_dim.156), calls=%async_computation.1 | async-start | bytes 262144 | tf_op jit(solution)/shard_map/all_to_all | solution.py:19
  50.0 10.9 %all-to-all-start.2 = ((f32[8,1,4096]{2,1,0:T(1,128)}), f32[8,1,4096]{2,1,0:T(1,128)S(1)}, u32[]{:S(2)}, u32[]{:S(2)}) async-start(f32[8,1,4096]{2,1,0:T(1,128)} %broadcast_in_dim.158), calls=%async_computation.2 | async-start | bytes 262144 | tf_op jit(solution)/shard_map/all_to_all | solution.py:19
  69.4 10.7 %all-to-all-start.3 = ((f32[8,1,4096]{2,1,0:T(1,128)}), f32[8,1,4096]{2,1,0:T(1,128)S(1)}, u32[]{:S(2)}, u32[]{:S(2)}) async-start(f32[8,1,4096]{2,1,0:T(1,128)} %broadcast_in_dim.160), calls=%async_computation.3 | async-start | bytes 262144 | tf_op jit(solution)/shard_map/all_to_all | solution.py:19
  88.6 10.7 %all-to-all-start.4 = ((f32[8,1,4096]{2,1,0:T(1,128)}), f32[8,1,4096]{2,1,0:T(1,128)S(1)}, u32[]{:S(2)}, u32[]{:S(2)}) async-start(f32[8,1,4096]{2,1,0:T(1,128)} %broadcast_in_dim.162), calls=%async_computation.4 | async-start | bytes 262144 | tf_op jit(solution)/shard_map/all_to_all | solution.py:19
  107.8 11.1 %all-to-all-start.5 = ((f32[8,1,4096]{2,1,0:T(1,128)}), f32[8,1,4096]{2,1,0:T(1,128)S(1)}, u32[]{:S(2)}, u32[]{:S(2)}) async-start(f32[8,1,4096]{2,1,0:T(1,128)} %broadcast_in_dim.164), calls=%async_computation.5 | async-start | bytes 262144 | tf_op jit(solution)/shard_map/all_to_all | solution.py:19
  127.4 10.7 %all-to-all-start.6 = ((f32[8,1,4096]{2,1,0:T(1,128)}), f32[8,1,4096]{2,1,0:T(1,128)S(1)}, u32[]{:S(2)}, u32[]{:S(2)}) async-start(f32[8,1,4096]{2,1,0:T(1,128)} %broadcast_in_dim.166), calls=%async_computation.6 | async-start | bytes 262144 | tf_op jit(solution)/shard_map/all_to_all | solution.py:19
  145.0 24.3 %copy-start.3 = (f32[4,1,4096]{2,1,0:T(1,128)S(1)}, f32[4,1,4096]{2,1,0:T(1,128)}, u32[]{:S(2)}) copy-start(f32[4,1,4096]{2,1,0:T(1,128)} %param.11) | copy-start | bytes 196612
  146.6 10.7 %all-to-all-start.7 = ((f32[8,1,4096]{2,1,0:T(1,128)}), f32[8,1,4096]{2,1,0:T(1,128)S(1)}, u32[]{:S(2)}, u32[]{:S(2)}) async-start(f32[8,1,4096]{2,1,0:T(1,128)} %broadcast_in_dim.168), calls=%async_computation.7 | async-start | bytes 262144 | tf_op jit(solution)/shard_map/all_to_all | solution.py:19
  158.4 20.7 %slice-start.1 = ((f32[1,2,64]{2,1,0:T(2,128)}), f32[1,1,64]{2,1,0:T(1,128)S(1)}, s32[]{:S(2)}) async-start(f32[1,2,64]{2,1,0:T(2,128)} %param.14), calls=%async_computation.34 | async-start | bytes 1024 | tf_op jit(solution)/shard_map/slice | solution.py:31
  158.4 22.1 %copy-start.4 = (f32[1,64]{1,0:T(1,128)S(1)}, f32[1,64]{1,0:T(1,128)}, u32[]{:S(2)}) copy-start(f32[1,64]{1,0:T(1,128)} %param.15) | copy-start | bytes 772
  158.4 22.1 %copy-start.5 = (f32[1,2,64]{2,1,0:T(2,128)S(1)}, f32[1,2,64]{2,1,0:T(2,128)}, u32[]{:S(2)}) copy-start(f32[1,2,64]{2,1,0:T(2,128)} %param.14) | copy-start | bytes 1540
  165.8 10.8 %all-to-all-start.8 = ((f32[8,1,4096]{2,1,0:T(1,128)}), f32[8,1,4096]{2,1,0:T(1,128)S(1)}, u32[]{:S(2)}, u32[]{:S(2)}) async-start(f32[8,1,4096]{2,1,0:T(1,128)} %broadcast_in_dim.170), calls=%async_computation.8 | async-start | bytes 262144 | tf_op jit(solution)/shard_map/all_to_all | solution.py:19
  179.1 1.4 collective-permute-start.1
  180.4 7.4 %collective-permute-start = (f32[1,64]{1,0:T(1,128)S(1)}, f32[1,64]{1,0:T(1,128)S(1)}, u32[]{:S(2)}, u32[]{:S(2)}) collective-permute-start(f32[1,64]{1,0:T(1,128)S(1)} %get-tuple-element.85), channel_id=1, source_target_pairs={{0,8},{8,16},{16,24},{24,0},{1,9},{9,17},{17,25},{25,1},{2,10},{10... | collective-permute-start | bytes 776 | tf_op jit(solution)/shard_map/ppermute | solution.py:13
  190.9 10.8 %all-to-all-start.9 = ((f32[8,1,4096]{2,1,0:T(1,128)}), f32[8,1,4096]{2,1,0:T(1,128)S(1)}, u32[]{:S(2)}, u32[]{:S(2)}) async-start(f32[8,1,4096]{2,1,0:T(1,128)} %broadcast_in_dim.173), calls=%async_computation.9 | async-start | bytes 262144 | tf_op jit(solution)/shard_map/all_to_all | solution.py:19
  210.2 10.9 %all-to-all-start.10 = ((f32[8,1,4096]{2,1,0:T(1,128)}), f32[8,1,4096]{2,1,0:T(1,128)S(1)}, u32[]{:S(2)}, u32[]{:S(2)}) async-start(f32[8,1,4096]{2,1,0:T(1,128)} %broadcast_in_dim.175), calls=%async_computation.10 | async-start | bytes 262144 | tf_op jit(solution)/shard_map/all_to_all | solution.py:19
  229.6 10.7 %all-to-all-start.11 = ((f32[8,1,4096]{2,1,0:T(1,128)}), f32[8,1,4096]{2,1,0:T(1,128)S(1)}, u32[]{:S(2)}, u32[]{:S(2)}) async-start(f32[8,1,4096]{2,1,0:T(1,128)} %broadcast_in_dim.177), calls=%async_computation.11 | async-start | bytes 262144 | tf_op jit(solution)/shard_map/all_to_all | solution.py:19
  248.8 10.7 %all-to-all-start.12 = ((f32[8,1,4096]{2,1,0:T(1,128)}), f32[8,1,4096]{2,1,0:T(1,128)S(1)}, u32[]{:S(2)}, u32[]{:S(2)}) async-start(f32[8,1,4096]{2,1,0:T(1,128)} %broadcast_in_dim.179), calls=%async_computation.12 | async-start | bytes 262144 | tf_op jit(solution)/shard_map/all_to_all | solution.py:19
  268.0 11.1 %all-to-all-start.13 = ((f32[8,1,4096]{2,1,0:T(1,128)}), f32[8,1,4096]{2,1,0:T(1,128)S(1)}, u32[]{:S(2)}, u32[]{:S(2)}) async-start(f32[8,1,4096]{2,1,0:T(1,128)} %broadcast_in_dim.181), calls=%async_computation.13 | async-start | bytes 262144 | tf_op jit(solution)/shard_map/all_to_all | solution.py:19
  287.6 10.7 %all-to-all-start.14 = ((f32[8,1,4096]{2,1,0:T(1,128)}), f32[8,1,4096]{2,1,0:T(1,128)S(1)}, u32[]{:S(2)}, u32[]{:S(2)}) async-start(f32[8,1,4096]{2,1,0:T(1,128)} %broadcast_in_dim.359), calls=%async_computation.14 | async-start | bytes 262144 | tf_op jit(solution)/shard_map/all_to_all | solution.py:19
  306.8 10.7 %all-to-all-start.15 = ((f32[8,1,4096]{2,1,0:T(1,128)}), f32[8,1,4096]{2,1,0:T(1,128)S(1)}, u32[]{:S(2)}, u32[]{:S(2)}) async-start(f32[8,1,4096]{2,1,0:T(1,128)} %broadcast_in_dim.361), calls=%async_computation.15 | async-start | bytes 262144 | tf_op jit(solution)/shard_map/all_to_all | solution.py:19
  326.0 10.8 %all-to-all-start.16 = ((f32[8,1,4096]{2,1,0:T(1,128)}), f32[8,1,4096]{2,1,0:T(1,128)S(1)}, u32[]{:S(2)}, u32[]{:S(2)}) async-start(f32[8,1,4096]{2,1,0:T(1,128)} %broadcast_in_dim.363), calls=%async_computation.16 | async-start | bytes 262144 | tf_op jit(solution)/shard_map/all_to_all | solution.py:19
  339.2 1.4 collective-permute-start.3
  340.6 6.5 collective-permute-start.2
  350.0 10.8 %all-to-all-start.17 = ((f32[8,1,4096]{2,1,0:T(1,128)}), f32[8,1,4096]{2,1,0:T(1,128)S(1)}, u32[]{:S(2)}, u32[]{:S(2)}) async-start(f32[8,1,4096]{2,1,0:T(1,128)} %broadcast_in_dim.366), calls=%async_computation.17 | async-start | bytes 262144 | tf_op jit(solution)/shard_map/all_to_all | solution.py:19
  369.3 10.9 %all-to-all-start.18 = ((f32[8,1,4096]{2,1,0:T(1,128)}), f32[8,1,4096]{2,1,0:T(1,128)S(1)}, u32[]{:S(2)}, u32[]{:S(2)}) async-start(f32[8,1,4096]{2,1,0:T(1,128)} %broadcast_in_dim.368), calls=%async_computation.18 | async-start | bytes 262144 | tf_op jit(solution)/shard_map/all_to_all | solution.py:19
  388.7 10.7 %all-to-all-start.19 = ((f32[8,1,4096]{2,1,0:T(1,128)}), f32[8,1,4096]{2,1,0:T(1,128)S(1)}, u32[]{:S(2)}, u32[]{:S(2)}) async-start(f32[8,1,4096]{2,1,0:T(1,128)} %broadcast_in_dim.370), calls=%async_computation.19 | async-start | bytes 262144 | tf_op jit(solution)/shard_map/all_to_all | solution.py:19
  407.9 10.7 %all-to-all-start.20 = ((f32[8,1,4096]{2,1,0:T(1,128)}), f32[8,1,4096]{2,1,0:T(1,128)S(1)}, u32[]{:S(2)}, u32[]{:S(2)}) async-start(f32[8,1,4096]{2,1,0:T(1,128)} %broadcast_in_dim.372), calls=%async_computation.20 | async-start | bytes 262144 | tf_op jit(solution)/shard_map/all_to_all | solution.py:19
  427.1 11.1 %all-to-all-start.21 = ((f32[8,1,4096]{2,1,0:T(1,128)}), f32[8,1,4096]{2,1,0:T(1,128)S(1)}, u32[]{:S(2)}, u32[]{:S(2)}) async-start(f32[8,1,4096]{2,1,0:T(1,128)} %broadcast_in_dim.374), calls=%async_computation.21 | async-start | bytes 262144 | tf_op jit(solution)/shard_map/all_to_all | solution.py:19
  446.7 10.7 %all-to-all-start.22 = ((f32[8,1,4096]{2,1,0:T(1,128)}), f32[8,1,4096]{2,1,0:T(1,128)S(1)}, u32[]{:S(2)}, u32[]{:S(2)}) async-start(f32[8,1,4096]{2,1,0:T(1,128)} %broadcast_in_dim.376), calls=%async_computation.22 | async-start | bytes 262144 | tf_op jit(solution)/shard_map/all_to_all | solution.py:19
  465.9 10.7 %all-to-all-start.23 = ((f32[8,1,4096]{2,1,0:T(1,128)}), f32[8,1,4096]{2,1,0:T(1,128)S(1)}, u32[]{:S(2)}, u32[]{:S(2)}) async-start(f32[8,1,4096]{2,1,0:T(1,128)} %broadcast_in_dim.378), calls=%async_computation.23 | async-start | bytes 262144 | tf_op jit(solution)/shard_map/all_to_all | solution.py:19
  485.1 10.8 %all-to-all-start.24 = ((f32[8,1,4096]{2,1,0:T(1,128)}), f32[8,1,4096]{2,1,0:T(1,128)S(1)}, u32[]{:S(2)}, u32[]{:S(2)}) async-start(f32[8,1,4096]{2,1,0:T(1,128)} %broadcast_in_dim.380), calls=%async_computation.24 | async-start | bytes 262144 | tf_op jit(solution)/shard_map/all_to_all | solution.py:19
  498.4 1.4 collective-permute-start.5
  499.7 7.4 %collective-permute-start.4 = (f32[1,64]{1,0:T(1,128)S(1)}, f32[1,64]{1,0:T(1,128)S(1)}, u32[]{:S(2)}, u32[]{:S(2)}) collective-permute-start(f32[1,64]{1,0:T(1,128)S(1)} %get-tuple-element.81), channel_id=1, source_target_pairs={{0,8},{8,16},{16,24},{24,0},{1,9},{9,17},{17,25},{25,1},{2,10},{10... | collective-permute-start | bytes 776 | tf_op jit(solution)/shard_map/ppermute | solution.py:13
  510.2 10.8 %all-to-all-start.25 = ((f32[8,1,4096]{2,1,0:T(1,128)}), f32[8,1,4096]{2,1,0:T(1,128)S(1)}, u32[]{:S(2)}, u32[]{:S(2)}) async-start(f32[8,1,4096]{2,1,0:T(1,128)} %broadcast_in_dim.383), calls=%async_computation.25 | async-start | bytes 262144 | tf_op jit(solution)/shard_map/all_to_all | solution.py:19
  529.5 10.9 %all-to-all-start.26 = ((f32[8,1,4096]{2,1,0:T(1,128)}), f32[8,1,4096]{2,1,0:T(1,128)S(1)}, u32[]{:S(2)}, u32[]{:S(2)}) async-start(f32[8,1,4096]{2,1,0:T(1,128)} %broadcast_in_dim.385), calls=%async_computation.26 | async-start | bytes 262144 | tf_op jit(solution)/shard_map/all_to_all | solution.py:19
  548.9 10.7 %all-to-all-start.27 = ((f32[8,1,4096]{2,1,0:T(1,128)}), f32[8,1,4096]{2,1,0:T(1,128)S(1)}, u32[]{:S(2)}, u32[]{:S(2)}) async-start(f32[8,1,4096]{2,1,0:T(1,128)} %broadcast_in_dim.387), calls=%async_computation.27 | async-start | bytes 262144 | tf_op jit(solution)/shard_map/all_to_all | solution.py:19
  568.0 10.7 %all-to-all-start.28 = ((f32[8,1,4096]{2,1,0:T(1,128)}), f32[8,1,4096]{2,1,0:T(1,128)S(1)}, u32[]{:S(2)}, u32[]{:S(2)}) async-start(f32[8,1,4096]{2,1,0:T(1,128)} %broadcast_in_dim.389), calls=%async_computation.28 | async-start | bytes 262144 | tf_op jit(solution)/shard_map/all_to_all | solution.py:19
  587.2 10.9 %all-to-all-start.29 = ((f32[8,1,4096]{2,1,0:T(1,128)}), f32[8,1,4096]{2,1,0:T(1,128)S(1)}, u32[]{:S(2)}, u32[]{:S(2)}) async-start(f32[8,1,4096]{2,1,0:T(1,128)} %broadcast_in_dim.391), calls=%async_computation.29 | async-start | bytes 262144 | tf_op jit(solution)/shard_map/all_to_all | solution.py:19
  606.7 10.7 %all-to-all-start.30 = ((f32[8,1,4096]{2,1,0:T(1,128)}), f32[8,1,4096]{2,1,0:T(1,128)S(1)}, u32[]{:S(2)}, u32[]{:S(2)}) async-start(f32[8,1,4096]{2,1,0:T(1,128)} %broadcast_in_dim.393), calls=%async_computation.30 | async-start | bytes 262144 | tf_op jit(solution)/shard_map/all_to_all | solution.py:19
  625.9 10.7 %all-to-all-start.31 = ((f32[8,1,4096]{2,1,0:T(1,128)}), f32[8,1,4096]{2,1,0:T(1,128)S(1)}, u32[]{:S(2)}, u32[]{:S(2)}) async-start(f32[8,1,4096]{2,1,0:T(1,128)} %broadcast_in_dim.395), calls=%async_computation.31 | async-start | bytes 262144 | tf_op jit(solution)/shard_map/all_to_all | solution.py:19
  643.7 16.4 %copy-start = (f32[1,4096]{1,0:T(1,128)}, f32[1,4096]{1,0:T(1,128)S(1)}, u32[]{:S(2)}) copy-start(f32[1,4096]{1,0:T(1,128)S(1)} %divide_add_fusion) | copy-start | bytes 49156
  655.2 1.4 collective-permute-start.7
  656.6 3.0 collective-permute-start.6
